TPU v7x, 128 devices: a whole 4x4x4 slice. The times are simulated.
128 devices in a mesh: af: 128 (over z, x, y, core).
Axes of the slice: x: 4, y: 4, z: 4, core: 2. Of those that a mesh axis runs over, the one named last changes fastest.
Arguments:
- reflection: bfloat16 [2, 256, 1536, 1536], P(None, 'af'), may hold values from -0.15625 to 0.15625
- focus_plus: float32 [32, 1536, 512], P(None, 'af'), may hold values from -6 to 6
- focus_direct: float32 [32, 1536, 512], P(None, 'af'), may hold values from -6 to 6
- onset_index: int32 [32, 1536], P(None, 'af'), may hold values from 64 to 256
Outputs:
- focus_minus: float32 [32, 1536, 512], P(None, 'af')
- focus_next: float32 [32, 1536, 512], P(None, 'af')
Inputs may be any that keep to these rules, and one draw needn't show every extreme that they name: onset_index[p, r] is the half-width in samples, around sample 512/2, of the window of focal point p at station r.
All inputs are finite; a program needn't handle non-finite values.
Results may differ from a plain program's by a relative error of at most 0.0029.
Values may be sent and summed in bfloat16 or wider, within the bound.
No kernel may reach another device: no remote copies, remote signals or barrier semaphores. Data moves between devices by JAX's collectives and lax.ppermute only.
A program may use at most 128 MiB of HBM per device.

v0:
```python
import math

import numpy as np

import jax
import jax.numpy as jnp
from jax import lax
from jax.sharding import PartitionSpec as P

NFREQ = 256
NT = 512


def base_table(nfreq, ntime):
    phase = (np.arange(nfreq)[:, None] * np.arange(ntime)[None, :]) % ntime
    angle = phase.astype(np.float64) * (2.0 * math.pi / ntime)
    table = np.stack([np.cos(angle), -np.sin(angle)], 1).reshape(2 * nfreq, ntime)
    return jnp.asarray(table.astype(np.float32))


def spectra_of(traces, table, groups):
    points, stations_dev, ntime = traces.shape
    mixed = lax.dot_general(
        traces,
        table,
        (((2,), (1,)), ((), ())),
        precision=lax.Precision.HIGHEST,
        preferred_element_type=jnp.float32,
    )
    scaled = (mixed * (1.0 / math.sqrt(ntime))).astype(jnp.bfloat16)
    local = table.shape[0] // 2 // groups
    scaled = scaled.reshape(points, stations_dev, groups, local, 2)
    scaled = scaled.transpose(2, 1, 3, 4, 0)
    return scaled.reshape(groups, stations_dev, local * 2 * points)


def traces_of(arrived, table, points):
    groups, stations_dev, lanes = arrived.shape
    local = lanes // (2 * points)
    spec = arrived.reshape(groups, stations_dev, local, 2, points)
    tab = table.reshape(groups, local, 2, table.shape[1])
    mixed = lax.dot_general(
        spec,
        tab,
        (((0, 2, 3), (0, 1, 2)), ((), ())),
        precision=lax.Precision.HIGHEST,
        preferred_element_type=jnp.float32,
    )
    scaled = mixed * (1.0 / math.sqrt(table.shape[0] // 2))
    return scaled.transpose(1, 0, 2)


def windowed(traces, onset_index):
    time_index = jnp.arange(traces.shape[2], dtype=jnp.int32)
    distance = jnp.abs(time_index - traces.shape[2] // 2)
    keep = distance[None, None, :] < onset_index[:, :, None]
    return jnp.where(keep, traces, jnp.zeros_like(traces))


def split_spectra(arrived, points):
    groups, stations_dev, lanes = arrived.shape
    local = lanes // (2 * points)
    spec = arrived.reshape(groups * stations_dev, local, 2, points).transpose(1, 0, 2, 3)
    real = spec[:, :, 0]
    imag = spec[:, :, 1]
    return real, imag, local


def forward_product(reflection, arrived, points):
    real, imag, local = split_spectra(arrived, points)
    both = jnp.concatenate([real, imag], 2)
    turned = jnp.concatenate([-imag, real], 2)
    out = jnp.einsum("ksr,krq->ksq", reflection[0], both, preferred_element_type=jnp.float32)
    out = out + jnp.einsum("ksr,krq->ksq", reflection[1], turned, preferred_element_type=jnp.float32)
    return out


def adjoint_product(reflection, arrived, points):
    real, imag, local = split_spectra(arrived, points)
    both = jnp.concatenate([real, imag], 2)
    turned = jnp.concatenate([imag, -real], 2)
    out = jnp.einsum("ksr,ksq->krq", reflection[0], both, preferred_element_type=jnp.float32)
    out = out + jnp.einsum("ksr,ksq->krq", reflection[1], turned, preferred_element_type=jnp.float32)
    return out


def to_owners(product, groups):
    local, stations, lanes = product.shape
    out = product.transpose(1, 0, 2).reshape(groups, stations // groups, local * lanes)
    return out


def per_device(reflection, focus_plus, focus_direct, onset_index):
    groups = lax.axis_size("af")
    points = focus_plus.shape[0]
    table = base_table(NFREQ, NT)

    def convolve(spectra, product):
        arrived = lax.all_to_all(spectra, "af", 0, 0, tiled=True)
        result = to_owners(product(reflection, arrived, points), groups)
        return lax.all_to_all(result, "af", 0, 0, tiled=True)

    images = convolve(spectra_of(focus_plus, table, groups), forward_product)
    focus_minus = windowed(traces_of(images, table, points), onset_index)
    returns = convolve(spectra_of(focus_minus, table, groups), adjoint_product)
    focus_next = focus_direct + windowed(traces_of(returns, table, points), onset_index)
    return (focus_minus, focus_next)


def solution(mesh):
    return jax.shard_map(
        per_device,
        mesh=mesh,
        in_specs=(
            P(None, "af", None, None),
            P(None, "af", None),
            P(None, "af", None),
            P(None, "af"),
        ),
        out_specs=(P(None, "af", None), P(None, "af", None)),
        check_vma=False,
    )
```

profile of v0, /device:TPU:1, one launch (start us, length us, event | category | flops | bytes accessed | tf_op | source)
XLA Modules:
  0.0 145.2 jit_solution(16241212814362603186)
XLA Ops:
  0.6 0.0 copy-start
  0.6 1.1 copy-done
  1.8 2.7 %fusion.57 = bf16[32,12,512]{2,0,1:T(8,128)(2,1)S(1)} fusion(f32[512,512,1]{1,0,2:T(8,128)} %constant.17, f32[32,12,512]{2,0,1:T(8,128)S(1)} %copy-done), kind=kOutput, calls=%fused_computation.33 | convolution fusion | flops 1208352768 | bytes 2228224 | tf_op jit(solution)/shard_map/dot_general | solution.py:23
  4.5 0.8 copy.31
  5.3 0.9 copy.32
  6.2 0.4 copy.33
  6.7 24.8 %all_to_all.20 = bf16[128,12,128]{2,1,0:T(8,128)(2,1)S(1)} all-to-all(bf16[128,12,128]{2,1,0:T(8,128)(2,1)S(1)} %copy.33), channel_id=1, replica_groups=mesh['af'=128] {'af'}, dimensions={0} | all-to-all | bytes 786432 | tf_op jit(solution)/shard_map/all_to_all | solution.py:99
  31.5 0.7 reshape.46
  32.2 2.0 %copy.34 = bf16[1536,2,2,32]{0,3,1,2:T(8,128)(2,1)S(1)} copy(bf16[1536,2,2,32]{3,2,1,0:T(2,128)(2,1)S(1)} %reshape.46) | data formatting | bytes 786432 | tf_op jit(solution)/shard_map/reshape | solution.py:63
  34.2 5.4 %fusion.2 = f32[2,64,1536]{2,1,0:T(8,128)S(1)} fusion(bf16[2,2,1536,1536]{3,2,1,0:T(8,128)(2,1)} %param.5, bf16[2,1536,32]{1,2,0:T(8,128)(2,1)S(1)} %get-tuple-element.5, bf16[2,1536,32]{1,2,0:T(8,128)(2,1)S(1)} %fusion.74), kind=kOutput, calls=%fused_computation.2 | convolution fusion | flops 604766208 | bytes 10616832 | tf_op jit(solution)/shard_map/ksr,krq->ksq/dot_general | solution.py:74
  39.7 7.6 %fusion.21 = f32[1536,2,64]{0,2,1:T(8,128)} fusion(f32[2,64,1536]{2,1,0:T(8,128)S(1)} %fusion.2, bf16[2,2,1536,1536]{3,2,1,0:T(8,128)(2,1)} %param.5, bf16[2,1536,32]{1,2,0:T(8,128)(2,1)S(1)} %get-tuple-element.4, bf16[2,1536,32]{1,2,0:T(8,128)(2,1)S(1)} %get-tuple-element.5), kind=kOutput, calls=%fused_computation.15 | convolution fusion | flops 604962816 | bytes 11403264 | tf_op jit(solution)/shard_map/ksr,krq->ksq/dot_general | solution.py:73
  47.3 2.4 %copy.35 = f32[1536,2,64]{2,1,0:T(2,128)S(1)} copy(f32[1536,2,64]{0,2,1:T(8,128)} %fusion.21) | data formatting | bytes 1572864 | tf_op jit(solution)/shard_map/add | solution.py:74
  49.7 1.9 %reshape.47 = f32[128,12,128]{2,1,0:T(8,128)} reshape(f32[1536,2,64]{2,1,0:T(2,128)S(1)} %copy.35) | data formatting | bytes 1572864 | tf_op jit(solution)/shard_map/reshape | solution.py:89
  51.6 4.5 %all-to-all-start.1 = ((f32[128,12,128]{2,1,0:T(8,128)}), f32[128,12,128]{2,1,0:T(8,128)S(1)}, u32[]{:S(2)}, u32[]{:S(2)}) async-start(f32[128,12,128]{2,1,0:T(8,128)} %reshape.47), calls=%async_computation.1 | async-start | bytes 2097152 | tf_op jit(solution)/shard_map/all_to_all | solution.py:101
  56.1 18.8 %all-to-all-done.1 = f32[128,12,128]{2,1,0:T(8,128)S(1)} async-done(((f32[128,12,128]{2,1,0:T(8,128)}), f32[128,12,128]{2,1,0:T(8,128)S(1)}, u32[]{:S(2)}, u32[]{:S(2)}) %all-to-all-start.1) | async-done | bytes 786464 | tf_op jit(solution)/shard_map/all_to_all | solution.py:101
  74.9 1.2 copy.36
  76.2 2.6 %fusion.37 = f32[32,12,512]{2,0,1:T(8,128)S(1)} fusion(f32[128,12,2,2,32]{0,4,3,2,1:T(8,128)} %bitcast.121, f32[128,2,2,512,1]{3,0,2,4,1:T(8,128)S(1)} %copy-done.1, s32[32,12]{0,1:T(8,128)S(1)} %copy-done.3, s32[512]{0:T(512)S(1)} %add_abs_fusion), kind=kOutput, calls=%fused_computation.25 | convolution fusion | flops 1208549376 | bytes 2625024 | tf_op jit(solution)/shard_map/dot_general | solution.py:42
  78.8 0.9 copy-done.2
  79.6 2.7 %fusion.56 = bf16[32,12,512]{2,0,1:T(8,128)(2,1)S(1)} fusion(f32[32,12,512]{2,0,1:T(8,128)S(1)} %fusion.37, f32[512,512,1]{1,0,2:T(8,128)} %constant.17), kind=kOutput, calls=%fused_computation.32 | convolution fusion | flops 1208352768 | bytes 2228224 | tf_op jit(solution)/shard_map/dot_general | solution.py:23
  82.3 0.8 copy.38
  83.1 0.9 copy.39
  84.1 0.4 copy.40
  84.5 18.0 %all_to_all.21 = bf16[128,12,128]{2,1,0:T(8,128)(2,1)S(1)} all-to-all(bf16[128,12,128]{2,1,0:T(8,128)(2,1)S(1)} %copy.40), channel_id=1, replica_groups=mesh['af'=128] {'af'}, dimensions={0} | all-to-all | bytes 786432 | tf_op jit(solution)/shard_map/all_to_all | solution.py:99
  102.6 0.7 reshape.52
  103.2 2.0 %copy.41 = bf16[1536,2,2,32]{0,3,1,2:T(8,128)(2,1)S(1)} copy(bf16[1536,2,2,32]{3,2,1,0:T(2,128)(2,1)S(1)} %reshape.52) | data formatting | bytes 786432 | tf_op jit(solution)/shard_map/reshape | solution.py:63
  105.3 5.4 %fusion = f32[2,64,1536]{2,1,0:T(8,128)S(1)} fusion(bf16[2,2,1536,1536]{3,2,1,0:T(8,128)(2,1)} %param.5, bf16[2,1536,32]{1,2,0:T(8,128)(2,1)S(1)} %fusion.75, bf16[2,1536,32]{1,2,0:T(8,128)(2,1)S(1)} %get-tuple-element.3), kind=kOutput, calls=%fused_computation | convolution fusion | flops 604766208 | bytes 10616832 | tf_op jit(solution)/shard_map/ksr,ksq->krq/dot_general | solution.py:83
  110.7 5.5 %fusion.18 = f32[1536,2,64]{0,2,1:T(8,128)S(1)} fusion(f32[2,64,1536]{2,1,0:T(8,128)S(1)} %fusion, bf16[2,2,1536,1536]{3,2,1,0:T(8,128)(2,1)} %param.5, bf16[2,1536,32]{1,2,0:T(8,128)(2,1)S(1)} %get-tuple-element.3, bf16[2,1536,32]{1,2,0:T(8,128)(2,1)S(1)} %get-tuple-element.2), kind=kOutput, calls=%fused_computation.14 | convolution fusion | flops 604962816 | bytes 11403264 | tf_op jit(solution)/shard_map/ksr,ksq->krq/dot_general | solution.py:82
  116.2 0.8 copy.42
  117.0 0.9 reshape.53
  117.9 23.1 %all_to_all.22 = f32[128,12,128]{2,1,0:T(8,128)S(1)} all-to-all(f32[128,12,128]{2,1,0:T(8,128)S(1)} %reshape.53), channel_id=1, replica_groups=mesh['af'=128] {'af'}, dimensions={0} | all-to-all | bytes 1572864 | tf_op jit(solution)/shard_map/all_to_all | solution.py:101
  141.0 0.3 copy.43
  141.4 3.8 %fusion.52 = f32[32,12,512]{2,0,1:T(8,128)} fusion(f32[32,12,512]{2,0,1:T(8,128)} %param.7, f32[128,12,2,2,32]{0,4,3,2,1:T(8,128)S(1)} %bitcast.120, f32[128,2,2,512,1]{3,0,2,4,1:T(8,128)} %constant.18, s32[32,12]{0,1:T(8,128)S(1)} %copy-done.3, s32[512]{0:T(512)S(1)} %add_abs_fusion), kind=kOutput, calls=%fused_computation.30 | convolution fusion | flops 1208745984 | bytes 3411456 | tf_op jit(solution)/shard_map/dot_general | solution.py:42
  (10 shorter events, 0.1 us)
Async XLA Ops:
  0.6 1.1 copy-start
  39.7 36.5 %copy-start.1 = (f32[128,2,2,512,1]{3,0,2,4,1:T(8,128)S(1)}, f32[128,2,2,512,1]{3,0,2,4,1:T(8,128)}, u32[]{:S(2)}) copy-start(f32[128,2,2,512,1]{3,0,2,4,1:T(8,128)} %constant.18) | copy-start | bytes 3145732
  39.7 36.5 %copy-start.3 = (s32[32,12]{0,1:T(8,128)S(1)}, s32[32,12]{0,1:T(8,128)}, u32[]{:S(2)}) copy-start(s32[32,12]{0,1:T(8,128)} %param.8) | copy-start | bytes 4612
  51.6 23.4 %all-to-all-start.1 = ((f32[128,12,128]{2,1,0:T(8,128)}), f32[128,12,128]{2,1,0:T(8,128)S(1)}, u32[]{:S(2)}, u32[]{:S(2)}) async-start(f32[128,12,128]{2,1,0:T(8,128)} %reshape.47), calls=%async_computation.1 | async-start | bytes 2097152 | tf_op jit(solution)/shard_map/all_to_all | solution.py:101
  78.7 0.9 copy-start.2
where the time goes:
time: 146 us; the launch traced here: 145 us
  blocking collectives  66 us (45%)
  matrix products  35.6 us (24%)
  local copies, waits for them, and re-layouts  19.3 us (13%)
  waiting for transfers between devices  18.8 us (13%)
  starting transfers between devices  4.51 us (3%)
    all_to_all x2, blocking collectives, convolve(): arrived = lax.all_to_all(spectra, 'af', 0, 0, tiled=True)  42.9 us
    all_to_all x1, blocking collectives, convolve(): return lax.all_to_all(result, 'af', 0, 0, tiled=True)  23.1 us
    all_to_all x1, waiting for transfers between devices, convolve(): return lax.all_to_all(result, 'af', 0, 0, tiled=True)  18.8 us
    dot_general x1, matrix products, forward_product(): jnp.einsum('ksr,krq->ksq', reflection[0], both, preferred_element_type=jn...  7.59 us
    dot_general x2, matrix products, traces_of(): lax.dot_general(spec, tab, (((0, 2, 3), (0, 1, 2)), ((), ())), precision=...  6.38 us
    dot_general x1, matrix products, adjoint_product(): jnp.einsum('ksr,ksq->krq', reflection[0], both, preferred_element_type=jn...  5.46 us
    dot_general x1, matrix products, adjoint_product(): jnp.einsum('ksr,ksq->krq', reflection[1], turned, preferred_element_type=...  5.43 us
    dot_general x1, matrix products, forward_product(): jnp.einsum('ksr,krq->ksq', reflection[1], turned, preferred_element_type=...  5.42 us
  transfers between devices with their start and end apart: 1, of which 1 were waited for; matrix products, arithmetic and copies ran while one was open for 0% of the time, Pallas kernels for 0%

commit v1 on v0

--- a/solution.py
+++ b/solution.py
@@ -5,10 +5,92 @@
 import jax
 import jax.numpy as jnp
 from jax import lax
+from jax.experimental import pallas as pl
+from jax.experimental.pallas import tpu as pltpu
 from jax.sharding import PartitionSpec as P
 
 NFREQ = 256
 NT = 512
+TS = 128
+
+
+def _fwd_kernel(x_ref, r_ref, o_ref, xp_ref):
+    @pl.when(pl.program_id(0) == 0)
+    def _():
+        x = x_ref[...].astype(jnp.float32)
+        lane = lax.broadcasted_iota(jnp.int32, x.shape, 1)
+        first = (lane % 64) < 32
+        xp = jnp.where(first, -pltpu.roll(x, 96, 1), pltpu.roll(x, 32, 1))
+        xp_ref[...] = xp.astype(jnp.bfloat16)
+
+    x = x_ref[...]
+    xp = xp_ref[...]
+    a0 = jnp.dot(r_ref[0, 0], x, preferred_element_type=jnp.float32)
+    a0 = a0 + jnp.dot(r_ref[1, 0], xp, preferred_element_type=jnp.float32)
+    a1 = jnp.dot(r_ref[0, 1], x, preferred_element_type=jnp.float32)
+    a1 = a1 + jnp.dot(r_ref[1, 1], xp, preferred_element_type=jnp.float32)
+    lane = lax.broadcasted_iota(jnp.int32, a0.shape, 1)
+    o_ref[...] = jnp.where(lane < 64, a0, a1)
+
+
+def forward_kernel(reflection, x):
+    stations = x.shape[0]
+    return pl.pallas_call(
+        _fwd_kernel,
+        grid=(stations // TS,),
+        in_specs=[
+            pl.BlockSpec((stations, 128), lambda i: (0, 0)),
+            pl.BlockSpec((2, 2, TS, stations), lambda i: (0, 0, i, 0)),
+        ],
+        out_specs=pl.BlockSpec((TS, 128), lambda i: (i, 0)),
+        out_shape=jax.ShapeDtypeStruct((stations, 128), jnp.float32),
+        scratch_shapes=[pltpu.VMEM((stations, 128), jnp.bfloat16)],
+    )(x, reflection)
+
+
+def _adj_kernel(y_ref, r_ref, o_ref, yt_ref, ytp_ref, acc_ref):
+    i = pl.program_id(0)
+
+    @pl.when(i == 0)
+    def _():
+        yt = y_ref[...].astype(jnp.float32).T
+        ytp = jnp.concatenate(
+            [yt[32:64], -yt[0:32], yt[96:128], -yt[64:96]], 0)
+        yt_ref[...] = yt.astype(jnp.bfloat16)
+        ytp_ref[...] = ytp.astype(jnp.bfloat16)
+        acc_ref[...] = jnp.zeros(acc_ref.shape, jnp.float32)
+
+    off = pl.multiple_of(i * TS, TS)
+    yt = yt_ref[:, pl.ds(off, TS)]
+    ytp = ytp_ref[:, pl.ds(off, TS)]
+    a0 = jnp.dot(yt[0:64], r_ref[0, 0], preferred_element_type=jnp.float32)
+    a0 = a0 + jnp.dot(ytp[0:64], r_ref[1, 0], preferred_element_type=jnp.float32)
+    a1 = jnp.dot(yt[64:128], r_ref[0, 1], preferred_element_type=jnp.float32)
+    a1 = a1 + jnp.dot(ytp[64:128], r_ref[1, 1], preferred_element_type=jnp.float32)
+    acc_ref[...] += jnp.concatenate([a0, a1], 0)
+
+    @pl.when(i == pl.num_programs(0) - 1)
+    def _():
+        o_ref[...] = acc_ref[...].T
+
+
+def adjoint_kernel(reflection, y):
+    stations = y.shape[0]
+    return pl.pallas_call(
+        _adj_kernel,
+        grid=(stations // TS,),
+        in_specs=[
+            pl.BlockSpec((stations, 128), lambda i: (0, 0)),
+            pl.BlockSpec((2, 2, TS, stations), lambda i: (0, 0, i, 0)),
+        ],
+        out_specs=pl.BlockSpec((stations, 128), lambda i: (0, 0)),
+        out_shape=jax.ShapeDtypeStruct((stations, 128), jnp.float32),
+        scratch_shapes=[
+            pltpu.VMEM((128, stations), jnp.bfloat16),
+            pltpu.VMEM((128, stations), jnp.bfloat16),
+            pltpu.VMEM((128, stations), jnp.float32),
+        ],
+    )(y, reflection)
 
 
 def base_table(nfreq, ntime):
@@ -57,39 +139,6 @@
     return jnp.where(keep, traces, jnp.zeros_like(traces))
 
 
-def split_spectra(arrived, points):
-    groups, stations_dev, lanes = arrived.shape
-    local = lanes // (2 * points)
-    spec = arrived.reshape(groups * stations_dev, local, 2, points).transpose(1, 0, 2, 3)
-    real = spec[:, :, 0]
-    imag = spec[:, :, 1]
-    return real, imag, local
-
-
-def forward_product(reflection, arrived, points):
-    real, imag, local = split_spectra(arrived, points)
-    both = jnp.concatenate([real, imag], 2)
-    turned = jnp.concatenate([-imag, real], 2)
-    out = jnp.einsum("ksr,krq->ksq", reflection[0], both, preferred_element_type=jnp.float32)
-    out = out + jnp.einsum("ksr,krq->ksq", reflection[1], turned, preferred_element_type=jnp.float32)
-    return out
-
-
-def adjoint_product(reflection, arrived, points):
-    real, imag, local = split_spectra(arrived, points)
-    both = jnp.concatenate([real, imag], 2)
-    turned = jnp.concatenate([imag, -real], 2)
-    out = jnp.einsum("ksr,ksq->krq", reflection[0], both, preferred_element_type=jnp.float32)
-    out = out + jnp.einsum("ksr,ksq->krq", reflection[1], turned, preferred_element_type=jnp.float32)
-    return out
-
-
-def to_owners(product, groups):
-    local, stations, lanes = product.shape
-    out = product.transpose(1, 0, 2).reshape(groups, stations // groups, local * lanes)
-    return out
-
-
 def per_device(reflection, focus_plus, focus_direct, onset_index):
     groups = lax.axis_size("af")
     points = focus_plus.shape[0]
@@ -97,12 +146,14 @@
 
     def convolve(spectra, product):
         arrived = lax.all_to_all(spectra, "af", 0, 0, tiled=True)
-        result = to_owners(product(reflection, arrived, points), groups)
+        stations = arrived.shape[0] * arrived.shape[1]
+        result = product(reflection, arrived.reshape(stations, arrived.shape[2]))
+        result = result.reshape(arrived.shape)
         return lax.all_to_all(result, "af", 0, 0, tiled=True)
 
-    images = convolve(spectra_of(focus_plus, table, groups), forward_product)
+    images = convolve(spectra_of(focus_plus, table, groups), forward_kernel)
     focus_minus = windowed(traces_of(images, table, points), onset_index)
-    returns = convolve(spectra_of(focus_minus, table, groups), adjoint_product)
+    returns = convolve(spectra_of(focus_minus, table, groups), adjoint_kernel)
     focus_next = focus_direct + windowed(traces_of(returns, table, points), onset_index)
     return (focus_minus, focus_next)
 

time: 146 us -> 146 us (level)
  Pallas kernels: 0 us -> 27.3 us
  matrix products: 35.6 us -> 9.89 us
  local copies, waits for them, and re-layouts: 19.3 us -> 17.6 us
    pallas_call x0 -> x2, Pallas kernels: none -> 27.3 us  [the longest x1 14.2 us: forward_kernel(): pl.pallas_call(_fwd_kernel, grid=(stations // TS,), in_specs=[pl.BlockSpe...]
    dot_general x4 -> x0, matrix products: 23.9 us -> none  [the longest x1 7.59 us: forward_product(): jnp.einsum('ksr,krq->ksq', reflection[0], both, preferred_element_type=jn...]
    add x2 -> x0, local copies, waits for them, and re-layouts: 3.21 us -> none  [the longest x1 2.39 us: forward_product(): out + jnp.einsum('ksr,krq->ksq', reflection[1], turned, preferred_element...]
    reshape x6 -> x4, local copies, waits for them, and re-layouts: 8.1 us -> 5.04 us  [the longest x2 3.37 us: convolve(): result = result.reshape(arrived.shape)]
    transpose x2, local copies, waits for them, and re-layouts: 1.86 us -> 3.4 us  [spectra_of(): scaled = scaled.transpose(2, 1, 3, 4, 0)]
where the time goes in v1:
time: 146 us; the launch traced here: 145 us
  blocking collectives  66.3 us (45%)
  Pallas kernels  27.3 us (19%)
  waiting for transfers between devices  18.9 us (13%)
  local copies, waits for them, and re-layouts  17.6 us (12%)
  matrix products  9.89 us (7%)
  starting transfers between devices  4.56 us (3%)
    all_to_all x2, blocking collectives, convolve(): arrived = lax.all_to_all(spectra, 'af', 0, 0, tiled=True)  42.9 us
    all_to_all x1, blocking collectives, convolve(): return lax.all_to_all(result, 'af', 0, 0, tiled=True)  23.4 us
    all_to_all x1, waiting for transfers between devices, convolve(): return lax.all_to_all(result, 'af', 0, 0, tiled=True)  18.9 us
    pallas_call x1, Pallas kernels, forward_kernel(): pl.pallas_call(_fwd_kernel, grid=(stations // TS,), in_specs=[pl.BlockSpe...  14.2 us
    pallas_call x1, Pallas kernels, adjoint_kernel(): pl.pallas_call(_adj_kernel, grid=(stations // TS,), in_specs=[pl.BlockSpe...  13.2 us
    dot_general x2, matrix products, traces_of(): lax.dot_general(spec, tab, (((0, 2, 3), (0, 1, 2)), ((), ())), precision=...  5.02 us
    dot_general x2, matrix products, spectra_of(): lax.dot_general(traces, table, (((2,), (1,)), ((), ())), precision=lax.Pr...  4.88 us
    all_to_all x1, starting transfers between devices, convolve(): return lax.all_to_all(result, 'af', 0, 0, tiled=True)  4.56 us
  transfers between devices with their start and end apart: 1, of which 1 were waited for; matrix products, arithmetic and copies ran while one was open for 0% of the time, Pallas kernels for 0%

profile of v1, /device:TPU:1, one launch (start us, length us, event | category | flops | bytes accessed | tf_op | source)
XLA Modules:
  0.0 145.4 jit_solution(16896453527665029586)
XLA Ops:
  0.6 0.0 copy-start
  0.6 1.1 copy-done
  1.8 2.7 %fusion.33 = bf16[32,12,512]{2,0,1:T(8,128)(2,1)S(1)} fusion(f32[512,512,1]{1,0,2:T(8,128)} %constant.17, f32[32,12,512]{2,0,1:T(8,128)S(1)} %copy-done), kind=kOutput, calls=%fused_computation.17 | convolution fusion | flops 1208352768 | bytes 2228224 | tf_op jit(solution)/shard_map/dot_general | solution.py:105
  4.5 0.8 copy.25
  5.3 0.9 copy.26
  6.2 0.4 copy.27
  6.7 24.8 %all_to_all.20 = bf16[128,12,128]{2,1,0:T(8,128)(2,1)S(1)} all-to-all(bf16[128,12,128]{2,1,0:T(8,128)(2,1)S(1)} %copy.27), channel_id=1, replica_groups=mesh['af'=128] {'af'}, dimensions={0} | all-to-all | bytes 786432 | tf_op jit(solution)/shard_map/all_to_all | solution.py:148
  31.5 0.8 reshape.46.x_ref
  32.3 14.2 %shard_map.68 = f32[1536,128]{1,0:T(8,128)} custom-call(bf16[1536,128]{1,0:T(8,128)(2,1)} %reshape.46.x_ref, bf16[2,2,1536,1536]{3,2,1,0:T(8,128)(2,1)} %r_ref.3), custom_call_target="tpu_custom_call" | custom-call | tf_op jit(solution)/shard_map/pallas_call | solution.py:38
  46.5 2.2 %reshape.47 = f32[128,12,128]{2,1,0:T(8,128)} reshape(f32[1536,128]{1,0:T(8,128)} %shard_map.68) | data formatting | bytes 1572864 | tf_op jit(solution)/shard_map/reshape | solution.py:151
  48.7 0.0 copy-start.1
  48.7 4.6 %all-to-all-start.1 = ((f32[128,12,128]{2,1,0:T(8,128)}), f32[128,12,128]{2,1,0:T(8,128)S(1)}, u32[]{:S(2)}, u32[]{:S(2)}) async-start(f32[128,12,128]{2,1,0:T(8,128)} %reshape.47), calls=%async_computation.1 | async-start | bytes 2097152 | tf_op jit(solution)/shard_map/all_to_all | solution.py:152
  53.3 18.9 %all-to-all-done.1 = f32[128,12,128]{2,1,0:T(8,128)S(1)} async-done(((f32[128,12,128]{2,1,0:T(8,128)}), f32[128,12,128]{2,1,0:T(8,128)S(1)}, u32[]{:S(2)}, u32[]{:S(2)}) %all-to-all-start.1) | async-done | bytes 786464 | tf_op jit(solution)/shard_map/all_to_all | solution.py:152
  72.2 1.2 copy.28
  73.4 0.0 copy-done.1
  73.4 0.0 copy-done.5
  73.4 2.7 %fusion.13 = f32[32,12,512]{2,0,1:T(8,128)S(1)} fusion(f32[128,12,2,2,32]{0,4,3,2,1:T(8,128)} %bitcast.85, f32[128,2,2,512,1]{3,0,2,4,1:T(8,128)S(1)} %copy-done.1, s32[32,12]{0,1:T(8,128)S(1)} %copy-done.5, s32[512]{0:T(512)S(1)} %add_abs_fusion), kind=kOutput, calls=%fused_computation.9 | convolution fusion | flops 1208549376 | bytes 2625024 | tf_op jit(solution)/shard_map/dot_general | solution.py:124
  76.1 0.0 copy-start.3
  76.1 0.9 copy-done.3
  77.0 0.0 copy-done.2
  77.0 2.2 %fusion.32 = bf16[32,12,512]{2,0,1:T(8,128)(2,1)} fusion(f32[32,12,512]{2,0,1:T(8,128)S(1)} %fusion.13, f32[512,512,1]{1,0,2:T(8,128)S(1)} %copy-done.2), kind=kOutput, calls=%fused_computation.16 | convolution fusion | flops 1208352768 | bytes 2228224 | tf_op jit(solution)/shard_map/dot_general | solution.py:105
  79.2 1.7 %copy.30 = bf16[32,12,512]{0,2,1:T(8,128)(2,1)S(1)} copy(bf16[32,12,512]{2,0,1:T(8,128)(2,1)} %fusion.32) | data formatting | bytes 786432 | tf_op jit(solution)/shard_map/convert_element_type | solution.py:112
  80.9 2.5 %copy.31 = bf16[128,12,2,2,32]{0,4,3,2,1:T(8,128)(2,1)} copy(bf16[128,12,2,2,32]{4,3,2,0,1:T(2,128)(2,1)S(1)} %bitcast.83) | data formatting | bytes 786432 | tf_op jit(solution)/shard_map/transpose | solution.py:115
  83.3 1.4 copy.32
  84.8 18.0 %all_to_all.21 = bf16[128,12,128]{2,1,0:T(8,128)(2,1)S(1)} all-to-all(bf16[128,12,128]{2,1,0:T(8,128)(2,1)S(1)} %copy.32), channel_id=1, replica_groups=mesh['af'=128] {'af'}, dimensions={0} | all-to-all | bytes 786432 | tf_op jit(solution)/shard_map/all_to_all | solution.py:148
  102.8 0.8 reshape.52.y_ref
  103.6 13.2 %shard_map.69 = f32[1536,128]{1,0:T(8,128)} custom-call(bf16[1536,128]{1,0:T(8,128)(2,1)} %reshape.52.y_ref, bf16[2,2,1536,1536]{3,2,1,0:T(8,128)(2,1)} %r_ref.3), custom_call_target="tpu_custom_call" | custom-call | tf_op jit(solution)/shard_map/pallas_call | solution.py:79
  116.8 1.2 reshape.53
  118.0 23.4 %all_to_all.22 = f32[128,12,128]{2,1,0:T(8,128)} all-to-all(f32[128,12,128]{2,1,0:T(8,128)S(1)} %reshape.53), channel_id=1, replica_groups=mesh['af'=128] {'af'}, dimensions={0} | all-to-all | bytes 1572864 | tf_op jit(solution)/shard_map/all_to_all | solution.py:152
  141.4 1.6 %copy.33 = f32[128,12,128]{0,2,1:T(8,128)S(1)} copy(f32[128,12,128]{2,1,0:T(8,128)} %all_to_all.22) | data formatting | bytes 1572864 | tf_op jit(solution)/shard_map/all_to_all | solution.py:152
  143.0 0.0 copy-done.4
  143.0 2.4 %fusion.28 = f32[32,12,512]{2,0,1:T(8,128)} fusion(f32[32,12,512]{2,0,1:T(8,128)S(1)} %copy-done.4, f32[128,12,2,2,32]{0,4,3,2,1:T(8,128)S(1)} %bitcast.84, f32[128,2,2,512,1]{3,0,2,4,1:T(8,128)S(1)} %copy-done.1, s32[32,12]{0,1:T(8,128)S(1)} %copy-done.5, s32[512]{0:T(512)S(1)} %add_abs_fusion), kind=kOutput, calls=%fused_computation.14 | convolution fusion | flops 1208745984 | bytes 3411456 | tf_op jit(solution)/shard_map/dot_general | solution.py:124
  (4 shorter events, 0.0 us)
Async XLA Ops:
  0.6 1.1 copy-start
  48.7 24.7 %copy-start.1 = (f32[128,2,2,512,1]{3,0,2,4,1:T(8,128)S(1)}, f32[128,2,2,512,1]{3,0,2,4,1:T(8,128)}, u32[]{:S(2)}) copy-start(f32[128,2,2,512,1]{3,0,2,4,1:T(8,128)} %constant.18) | copy-start | bytes 3145732
  48.7 24.7 %copy-start.5 = (s32[32,12]{0,1:T(8,128)S(1)}, s32[32,12]{0,1:T(8,128)}, u32[]{:S(2)}) copy-start(s32[32,12]{0,1:T(8,128)} %param.8) | copy-start | bytes 4612
  48.7 23.5 %all-to-all-start.1 = ((f32[128,12,128]{2,1,0:T(8,128)}), f32[128,12,128]{2,1,0:T(8,128)S(1)}, u32[]{:S(2)}, u32[]{:S(2)}) async-start(f32[128,12,128]{2,1,0:T(8,128)} %reshape.47), calls=%async_computation.1 | async-start | bytes 2097152 | tf_op jit(solution)/shard_map/all_to_all | solution.py:152
  73.4 3.6 %copy-start.2 = (f32[512,512,1]{1,0,2:T(8,128)S(1)}, f32[512,512,1]{1,0,2:T(8,128)}, u32[]{:S(2)}) copy-start(f32[512,512,1]{1,0,2:T(8,128)} %constant.17) | copy-start | bytes 3145732
  76.1 0.9 copy-start.3
  141.4 1.6 %copy-start.4 = (f32[32,12,512]{2,0,1:T(8,128)S(1)}, f32[32,12,512]{2,0,1:T(8,128)}, u32[]{:S(2)}) copy-start(f32[32,12,512]{2,0,1:T(8,128)} %param.7) | copy-start | bytes 2359300

commit v2 on v1

--- a/solution.py
+++ b/solution.py
@@ -11,26 +11,35 @@
 
 NFREQ = 256
 NT = 512
-TS = 128
+TS = 512
+
+
+def _partner(x, negate_first):
+    x = x.astype(jnp.float32)
+    lane = lax.broadcasted_iota(jnp.int32, x.shape, 1)
+    first = (lane % 64) < 32
+    ahead = pltpu.roll(x, 96, 1)
+    behind = pltpu.roll(x, 32, 1)
+    if negate_first:
+        out = jnp.where(first, -ahead, behind)
+    else:
+        out = jnp.where(first, ahead, -behind)
+    return out.astype(jnp.bfloat16)
 
 
 def _fwd_kernel(x_ref, r_ref, o_ref, xp_ref):
     @pl.when(pl.program_id(0) == 0)
     def _():
-        x = x_ref[...].astype(jnp.float32)
-        lane = lax.broadcasted_iota(jnp.int32, x.shape, 1)
-        first = (lane % 64) < 32
-        xp = jnp.where(first, -pltpu.roll(x, 96, 1), pltpu.roll(x, 32, 1))
-        xp_ref[...] = xp.astype(jnp.bfloat16)
+        xp_ref[...] = _partner(x_ref[...], True)
 
-    x = x_ref[...]
-    xp = xp_ref[...]
-    a0 = jnp.dot(r_ref[0, 0], x, preferred_element_type=jnp.float32)
-    a0 = a0 + jnp.dot(r_ref[1, 0], xp, preferred_element_type=jnp.float32)
-    a1 = jnp.dot(r_ref[0, 1], x, preferred_element_type=jnp.float32)
-    a1 = a1 + jnp.dot(r_ref[1, 1], xp, preferred_element_type=jnp.float32)
-    lane = lax.broadcasted_iota(jnp.int32, a0.shape, 1)
-    o_ref[...] = jnp.where(lane < 64, a0, a1)
+    parts = []
+    for kl in range(2):
+        x = x_ref[:, kl * 64:(kl + 1) * 64]
+        xp = xp_ref[:, kl * 64:(kl + 1) * 64]
+        a = jnp.dot(r_ref[0, kl], x, preferred_element_type=jnp.float32)
+        a = a + jnp.dot(r_ref[1, kl], xp, preferred_element_type=jnp.float32)
+        parts.append(a)
+    o_ref[...] = jnp.concatenate(parts, 1)
 
 
 def forward_kernel(reflection, x):
@@ -48,30 +57,30 @@
     )(x, reflection)
 
 
-def _adj_kernel(y_ref, r_ref, o_ref, yt_ref, ytp_ref, acc_ref):
+def _adj_kernel(y_ref, r_ref, o_ref, yp_ref, acc_ref):
     i = pl.program_id(0)
 
     @pl.when(i == 0)
     def _():
-        yt = y_ref[...].astype(jnp.float32).T
-        ytp = jnp.concatenate(
-            [yt[32:64], -yt[0:32], yt[96:128], -yt[64:96]], 0)
-        yt_ref[...] = yt.astype(jnp.bfloat16)
-        ytp_ref[...] = ytp.astype(jnp.bfloat16)
+        yp_ref[...] = _partner(y_ref[...], False)
         acc_ref[...] = jnp.zeros(acc_ref.shape, jnp.float32)
 
     off = pl.multiple_of(i * TS, TS)
-    yt = yt_ref[:, pl.ds(off, TS)]
-    ytp = ytp_ref[:, pl.ds(off, TS)]
-    a0 = jnp.dot(yt[0:64], r_ref[0, 0], preferred_element_type=jnp.float32)
-    a0 = a0 + jnp.dot(ytp[0:64], r_ref[1, 0], preferred_element_type=jnp.float32)
-    a1 = jnp.dot(yt[64:128], r_ref[0, 1], preferred_element_type=jnp.float32)
-    a1 = a1 + jnp.dot(ytp[64:128], r_ref[1, 1], preferred_element_type=jnp.float32)
-    acc_ref[...] += jnp.concatenate([a0, a1], 0)
+    y = y_ref[pl.ds(off, TS), :]
+    yp = yp_ref[pl.ds(off, TS), :]
+    dims = (((0,), (0,)), ((), ()))
+    parts = []
+    for kl in range(2):
+        a = lax.dot_general(r_ref[0, kl], y[:, kl * 64:(kl + 1) * 64], dims,
+                            preferred_element_type=jnp.float32)
+        a = a + lax.dot_general(r_ref[1, kl], yp[:, kl * 64:(kl + 1) * 64], dims,
+                                preferred_element_type=jnp.float32)
+        parts.append(a)
+    acc_ref[...] += jnp.concatenate(parts, 1)
 
     @pl.when(i == pl.num_programs(0) - 1)
     def _():
-        o_ref[...] = acc_ref[...].T
+        o_ref[...] = acc_ref[...]
 
 
 def adjoint_kernel(reflection, y):
@@ -86,9 +95,8 @@
         out_specs=pl.BlockSpec((stations, 128), lambda i: (0, 0)),
         out_shape=jax.ShapeDtypeStruct((stations, 128), jnp.float32),
         scratch_shapes=[
-            pltpu.VMEM((128, stations), jnp.bfloat16),
-            pltpu.VMEM((128, stations), jnp.bfloat16),
-            pltpu.VMEM((128, stations), jnp.float32),
+            pltpu.VMEM((stations, 128), jnp.bfloat16),
+            pltpu.VMEM((stations, 128), jnp.float32),
         ],
     )(y, reflection)
 

time: 146 us -> 140 us (0.959)
  Pallas kernels: 27.3 us -> 21.5 us
    pallas_call x1, Pallas kernels: 14.2 us -> 10.5 us  [forward_kernel(): pl.pallas_call(_fwd_kernel, grid=(stations // TS,), in_specs=[pl.BlockSpe...]
    pallas_call x1, Pallas kernels: 13.2 us -> 11 us  [adjoint_kernel(): pl.pallas_call(_adj_kernel, grid=(stations // TS,), in_specs=[pl.BlockSpe...]
where the time goes in v2:
time: 140 us; the launch traced here: 139 us
  blocking collectives  66.3 us (47%)
  Pallas kernels  21.5 us (15%)
  waiting for transfers between devices  18.9 us (13%)
  local copies, waits for them, and re-layouts  17.6 us (13%)
  matrix products  9.89 us (7%)
  starting transfers between devices  4.56 us (3%)
    all_to_all x2, blocking collectives, convolve(): arrived = lax.all_to_all(spectra, 'af', 0, 0, tiled=True)  42.9 us
    all_to_all x1, blocking collectives, convolve(): return lax.all_to_all(result, 'af', 0, 0, tiled=True)  23.4 us
    all_to_all x1, waiting for transfers between devices, convolve(): return lax.all_to_all(result, 'af', 0, 0, tiled=True)  18.9 us
    pallas_call x1, Pallas kernels, adjoint_kernel(): pl.pallas_call(_adj_kernel, grid=(stations // TS,), in_specs=[pl.BlockSpe...  11 us
    pallas_call x1, Pallas kernels, forward_kernel(): pl.pallas_call(_fwd_kernel, grid=(stations // TS,), in_specs=[pl.BlockSpe...  10.5 us
    dot_general x2, matrix products, traces_of(): lax.dot_general(spec, tab, (((0, 2, 3), (0, 1, 2)), ((), ())), precision=...  5.01 us
    dot_general x2, matrix products, spectra_of(): lax.dot_general(traces, table, (((2,), (1,)), ((), ())), precision=lax.Pr...  4.88 us
    all_to_all x1, starting transfers between devices, convolve(): return lax.all_to_all(result, 'af', 0, 0, tiled=True)  4.56 us
  transfers between devices with their start and end apart: 1, of which 1 were waited for; matrix products, arithmetic and copies ran while one was open for 0% of the time, Pallas kernels for 0%

profile of v2, /device:TPU:1, one launch (start us, length us, event | category | flops | bytes accessed | tf_op | source)
XLA Modules:
  0.0 139.5 jit_solution(988068736543985947)
XLA Ops:
  0.6 0.0 copy-start
  0.6 1.1 copy-done
  1.8 2.7 %fusion.33 = bf16[32,12,512]{2,0,1:T(8,128)(2,1)S(1)} fusion(f32[512,512,1]{1,0,2:T(8,128)} %constant.17, f32[32,12,512]{2,0,1:T(8,128)S(1)} %copy-done), kind=kOutput, calls=%fused_computation.17 | convolution fusion | flops 1208352768 | bytes 2228224 | tf_op jit(solution)/shard_map/dot_general | solution.py:113
  4.5 0.8 copy.25
  5.3 0.9 copy.26
  6.2 0.4 copy.27
  6.7 24.8 %all_to_all.20 = bf16[128,12,128]{2,1,0:T(8,128)(2,1)S(1)} all-to-all(bf16[128,12,128]{2,1,0:T(8,128)(2,1)S(1)} %copy.27), channel_id=1, replica_groups=mesh['af'=128] {'af'}, dimensions={0} | all-to-all | bytes 786432 | tf_op jit(solution)/shard_map/all_to_all | solution.py:156
  31.5 0.8 reshape.46.x_ref
  32.4 10.5 %shard_map.68 = f32[1536,128]{1,0:T(8,128)} custom-call(bf16[1536,128]{1,0:T(8,128)(2,1)} %reshape.46.x_ref, bf16[2,2,1536,1536]{3,2,1,0:T(8,128)(2,1)} %r_ref.3), custom_call_target="tpu_custom_call" | custom-call | tf_op jit(solution)/shard_map/pallas_call | solution.py:47
  42.8 2.2 %reshape.47 = f32[128,12,128]{2,1,0:T(8,128)} reshape(f32[1536,128]{1,0:T(8,128)} %shard_map.68) | data formatting | bytes 1572864 | tf_op jit(solution)/shard_map/reshape | solution.py:159
  45.0 0.0 copy-start.1
  45.0 4.6 %all-to-all-start.1 = ((f32[128,12,128]{2,1,0:T(8,128)}), f32[128,12,128]{2,1,0:T(8,128)S(1)}, u32[]{:S(2)}, u32[]{:S(2)}) async-start(f32[128,12,128]{2,1,0:T(8,128)} %reshape.47), calls=%async_computation.1 | async-start | bytes 2097152 | tf_op jit(solution)/shard_map/all_to_all | solution.py:160
  49.6 18.9 %all-to-all-done.1 = f32[128,12,128]{2,1,0:T(8,128)S(1)} async-done(((f32[128,12,128]{2,1,0:T(8,128)}), f32[128,12,128]{2,1,0:T(8,128)S(1)}, u32[]{:S(2)}, u32[]{:S(2)}) %all-to-all-start.1) | async-done | bytes 786464 | tf_op jit(solution)/shard_map/all_to_all | solution.py:160
  68.5 1.2 copy.28
  69.7 0.0 copy-done.1
  69.7 0.0 copy-done.5
  69.7 2.7 %fusion.13 = f32[32,12,512]{2,0,1:T(8,128)S(1)} fusion(f32[128,12,2,2,32]{0,4,3,2,1:T(8,128)} %bitcast.85, f32[128,2,2,512,1]{3,0,2,4,1:T(8,128)S(1)} %copy-done.1, s32[32,12]{0,1:T(8,128)S(1)} %copy-done.5, s32[512]{0:T(512)S(1)} %add_abs_fusion), kind=kOutput, calls=%fused_computation.9 | convolution fusion | flops 1208549376 | bytes 2625024 | tf_op jit(solution)/shard_map/dot_general | solution.py:132
  72.4 0.0 copy-start.3
  72.4 0.9 copy-done.3
  73.3 0.0 copy-done.2
  73.3 2.2 %fusion.32 = bf16[32,12,512]{2,0,1:T(8,128)(2,1)} fusion(f32[32,12,512]{2,0,1:T(8,128)S(1)} %fusion.13, f32[512,512,1]{1,0,2:T(8,128)S(1)} %copy-done.2), kind=kOutput, calls=%fused_computation.16 | convolution fusion | flops 1208352768 | bytes 2228224 | tf_op jit(solution)/shard_map/dot_general | solution.py:113
  75.5 1.7 %copy.30 = bf16[32,12,512]{0,2,1:T(8,128)(2,1)S(1)} copy(bf16[32,12,512]{2,0,1:T(8,128)(2,1)} %fusion.32) | data formatting | bytes 786432 | tf_op jit(solution)/shard_map/convert_element_type | solution.py:120
  77.2 2.5 %copy.31 = bf16[128,12,2,2,32]{0,4,3,2,1:T(8,128)(2,1)} copy(bf16[128,12,2,2,32]{4,3,2,0,1:T(2,128)(2,1)S(1)} %bitcast.83) | data formatting | bytes 786432 | tf_op jit(solution)/shard_map/transpose | solution.py:123
  79.7 1.4 %copy.32 = bf16[128,12,128]{2,1,0:T(8,128)(2,1)S(1)} copy(bf16[128,12,128]{0,2,1:T(8,128)(2,1)} %bitcast.87) | data formatting | bytes 786432 | tf_op jit(solution)/shard_map/reshape | solution.py:124
  81.1 18.0 %all_to_all.21 = bf16[128,12,128]{2,1,0:T(8,128)(2,1)S(1)} all-to-all(bf16[128,12,128]{2,1,0:T(8,128)(2,1)S(1)} %copy.32), channel_id=1, replica_groups=mesh['af'=128] {'af'}, dimensions={0} | all-to-all | bytes 786432 | tf_op jit(solution)/shard_map/all_to_all | solution.py:156
  99.1 0.8 reshape.52.y_ref
  100.0 11.0 %shard_map.69 = f32[1536,128]{1,0:T(8,128)} custom-call(bf16[1536,128]{1,0:T(8,128)(2,1)} %reshape.52.y_ref, bf16[2,2,1536,1536]{3,2,1,0:T(8,128)(2,1)} %r_ref.3), custom_call_target="tpu_custom_call" | custom-call | tf_op jit(solution)/shard_map/pallas_call | solution.py:88
  111.0 1.2 reshape.53
  112.2 23.4 %all_to_all.22 = f32[128,12,128]{2,1,0:T(8,128)} all-to-all(f32[128,12,128]{2,1,0:T(8,128)S(1)} %reshape.53), channel_id=1, replica_groups=mesh['af'=128] {'af'}, dimensions={0} | all-to-all | bytes 1572864 | tf_op jit(solution)/shard_map/all_to_all | solution.py:160
  135.5 1.6 %copy.33 = f32[128,12,128]{0,2,1:T(8,128)S(1)} copy(f32[128,12,128]{2,1,0:T(8,128)} %all_to_all.22) | data formatting | bytes 1572864 | tf_op jit(solution)/shard_map/all_to_all | solution.py:160
  137.1 0.0 copy-done.4
  137.1 2.4 %fusion.28 = f32[32,12,512]{2,0,1:T(8,128)} fusion(f32[32,12,512]{2,0,1:T(8,128)S(1)} %copy-done.4, f32[128,12,2,2,32]{0,4,3,2,1:T(8,128)S(1)} %bitcast.84, f32[128,2,2,512,1]{3,0,2,4,1:T(8,128)S(1)} %copy-done.1, s32[32,12]{0,1:T(8,128)S(1)} %copy-done.5, s32[512]{0:T(512)S(1)} %add_abs_fusion), kind=kOutput, calls=%fused_computation.14 | convolution fusion | flops 1208745984 | bytes 3411456 | tf_op jit(solution)/shard_map/dot_general | solution.py:132
  (4 shorter events, 0.0 us)
Async XLA Ops:
  0.6 1.1 copy-start
  45.0 24.7 %copy-start.1 = (f32[128,2,2,512,1]{3,0,2,4,1:T(8,128)S(1)}, f32[128,2,2,512,1]{3,0,2,4,1:T(8,128)}, u32[]{:S(2)}) copy-start(f32[128,2,2,512,1]{3,0,2,4,1:T(8,128)} %constant.18) | copy-start | bytes 3145732
  45.0 24.7 %copy-start.5 = (s32[32,12]{0,1:T(8,128)S(1)}, s32[32,12]{0,1:T(8,128)}, u32[]{:S(2)}) copy-start(s32[32,12]{0,1:T(8,128)} %param.8) | copy-start | bytes 4612
  45.0 23.5 %all-to-all-start.1 = ((f32[128,12,128]{2,1,0:T(8,128)}), f32[128,12,128]{2,1,0:T(8,128)S(1)}, u32[]{:S(2)}, u32[]{:S(2)}) async-start(f32[128,12,128]{2,1,0:T(8,128)} %reshape.47), calls=%async_computation.1 | async-start | bytes 2097152 | tf_op jit(solution)/shard_map/all_to_all | solution.py:160
  69.7 3.6 %copy-start.2 = (f32[512,512,1]{1,0,2:T(8,128)S(1)}, f32[512,512,1]{1,0,2:T(8,128)}, u32[]{:S(2)}) copy-start(f32[512,512,1]{1,0,2:T(8,128)} %constant.17) | copy-start | bytes 3145732
  72.4 0.9 copy-start.3
  135.5 1.6 %copy-start.4 = (f32[32,12,512]{2,0,1:T(8,128)S(1)}, f32[32,12,512]{2,0,1:T(8,128)}, u32[]{:S(2)}) copy-start(f32[32,12,512]{2,0,1:T(8,128)} %param.7) | copy-start | bytes 2359300

commit v3 on v2

--- a/solution.py
+++ b/solution.py
@@ -121,12 +121,13 @@
     local = table.shape[0] // 2 // groups
     scaled = scaled.reshape(points, stations_dev, groups, local, 2)
     scaled = scaled.transpose(2, 1, 3, 4, 0)
-    return scaled.reshape(groups, stations_dev, local * 2 * points)
+    return scaled.reshape(groups, 1, stations_dev * local * 2 * points)
 
 
 def traces_of(arrived, table, points):
-    groups, stations_dev, lanes = arrived.shape
-    local = lanes // (2 * points)
+    groups = arrived.shape[0]
+    stations_dev = arrived.size // (groups * 128)
+    local = 128 // (2 * points)
     spec = arrived.reshape(groups, stations_dev, local, 2, points)
     tab = table.reshape(groups, local, 2, table.shape[1])
     mixed = lax.dot_general(
@@ -154,8 +155,8 @@
 
     def convolve(spectra, product):
         arrived = lax.all_to_all(spectra, "af", 0, 0, tiled=True)
-        stations = arrived.shape[0] * arrived.shape[1]
-        result = product(reflection, arrived.reshape(stations, arrived.shape[2]))
+        stations = arrived.size // 128
+        result = product(reflection, arrived.reshape(stations, 128))
         result = result.reshape(arrived.shape)
         return lax.all_to_all(result, "af", 0, 0, tiled=True)
 

time: 140 us -> 135 us (0.964)
  other arithmetic: 0.01 us -> 7.63 us
  blocking collectives: 66.3 us -> 61 us
  local copies, waits for them, and re-layouts: 17.6 us -> 13.3 us
  waiting for transfers between devices: 18.9 us -> 16.3 us
    all_to_all x0 -> x2, other arithmetic: none -> 4.71 us  [convolve(): arrived = lax.all_to_all(spectra, 'af', 0, 0, tiled=True)]
    reshape x6 -> x3, local copies, waits for them, and re-layouts: 6.88 us -> 3.02 us  [the longest x2 2.42 us: convolve(): result = product(reflection, arrived.reshape(stations, 128))]
    reshape x0 -> x2, other arithmetic: none -> 2.92 us  [spectra_of(): return scaled.reshape(groups, 1, stations_dev * local * 2 * points)]
    all_to_all x2, blocking collectives: 42.9 us -> 40 us  [convolve(): arrived = lax.all_to_all(spectra, 'af', 0, 0, tiled=True)]
    all_to_all x1, waiting for transfers between devices: 18.9 us -> 16.3 us  [convolve(): return lax.all_to_all(result, 'af', 0, 0, tiled=True)]
    all_to_all x1, blocking collectives: 23.4 us -> 21 us  [convolve(): return lax.all_to_all(result, 'af', 0, 0, tiled=True)]
    all_to_all x2, local copies, waits for them, and re-layouts: 2.81 us -> 1.12 us  [convolve(): return lax.all_to_all(result, 'af', 0, 0, tiled=True)]
    unnamed x12 -> x16, local copies, waits for them, and re-layouts: 2.02 us -> 3.19 us
where the time goes in v3:
time: 135 us
  blocking collectives  61 us (45%)
  Pallas kernels  21.5 us (16%)
  waiting for transfers between devices  16.3 us (12%)
  local copies, waits for them, and re-layouts  13.3 us (10%)
  matrix products  9.81 us (7%)
  other arithmetic  7.63 us (6%)
  starting transfers between devices  4.55 us (3%)
    all_to_all x2, blocking collectives, convolve(): arrived = lax.all_to_all(spectra, 'af', 0, 0, tiled=True)  40 us
    all_to_all x1, blocking collectives, convolve(): return lax.all_to_all(result, 'af', 0, 0, tiled=True)  21 us
    all_to_all x1, waiting for transfers between devices, convolve(): return lax.all_to_all(result, 'af', 0, 0, tiled=True)  16.3 us
    pallas_call x1, Pallas kernels, adjoint_kernel(): pl.pallas_call(_adj_kernel, grid=(stations // TS,), in_specs=[pl.BlockSpe...  11 us
    pallas_call x1, Pallas kernels, forward_kernel(): pl.pallas_call(_fwd_kernel, grid=(stations // TS,), in_specs=[pl.BlockSpe...  10.5 us
    dot_general x2, matrix products, traces_of(): lax.dot_general(spec, tab, (((0, 2, 3), (0, 1, 2)), ((), ())), precision=...  4.93 us
    dot_general x2, matrix products, spectra_of(): lax.dot_general(traces, table, (((2,), (1,)), ((), ())), precision=lax.Pr...  4.88 us
    all_to_all x2, other arithmetic, convolve(): arrived = lax.all_to_all(spectra, 'af', 0, 0, tiled=True)  4.71 us
  transfers between devices with their start and end apart: 1, of which 1 were waited for; matrix products, arithmetic and copies ran while one was open for 0% of the time, Pallas kernels for 0%

profile of v3, /device:TPU:1, one launch (start us, length us, event | category | flops | bytes accessed | tf_op | source)
XLA Modules:
  0.0 134.8 jit_solution(13870852362794625040)
XLA Ops:
  0.6 1.1 copy-done
  1.8 2.7 %fusion.33 = bf16[32,12,512]{2,0,1:T(8,128)(2,1)S(1)} fusion(f32[512,512,1]{1,0,2:T(8,128)} %constant.17, f32[32,12,512]{2,0,1:T(8,128)S(1)} %copy-done), kind=kOutput, calls=%fused_computation.17 | convolution fusion | flops 1208352768 | bytes 2228224 | tf_op jit(solution)/shard_map/dot_general | solution.py:113
  4.5 0.8 copy.27
  5.3 0.9 copy.28
  6.2 0.6 broadcast.38
  6.8 1.0 reduce.2
  7.8 0.2 copy.42
  8.0 0.1 reshape.61
  8.1 23.5 %all_to_all.20 = bf16[128,2,768]{2,1,0:T(2,128)(2,1)S(1)} all-to-all(bf16[128,2,768]{2,1,0:T(2,128)(2,1)S(1)} %reshape.61), channel_id=1, replica_groups=mesh['af'=128] {'af'}, dimensions={0} | all-to-all | bytes 786432 | tf_op jit(solution)/shard_map/all_to_all | solution.py:157
  31.5 0.3 reshape.62
  31.9 2.4 %reduce = bf16[128,1536]{1,0:T(8,128)(2,1)S(1)} reduce(bf16[128,1,1536]{2,1,0:T(2,128)(2,1)S(1)} %reshape.62, bf16[]{:T(256)} %constant.19), dimensions={1}, to_apply=%all_to_all.12.reduce_sub_computation | reduce | bytes 786434 | tf_op jit(solution)/shard_map/all_to_all | solution.py:157
  34.2 1.2 reshape.46.x_ref
  35.4 10.5 %shard_map.68 = f32[1536,128]{1,0:T(8,128)} custom-call(bf16[1536,128]{1,0:T(8,128)(2,1)} %reshape.46.x_ref, bf16[2,2,1536,1536]{3,2,1,0:T(8,128)(2,1)} %r_ref.3), custom_call_target="tpu_custom_call" | custom-call | tf_op jit(solution)/shard_map/pallas_call | solution.py:47
  45.9 4.5 %all-to-all-start.1 = ((f32[128,1,1536]{2,1,0:T(1,128)}), f32[128,1,1536]{2,1,0:T(1,128)S(1)}, u32[]{:S(2)}, u32[]{:S(2)}) async-start(f32[128,1,1536]{2,1,0:T(1,128)} %bitcast.86), calls=%async_computation.1 | async-start | bytes 1572864 | tf_op jit(solution)/shard_map/all_to_all | solution.py:161
  50.5 16.3 %all-to-all-done.1 = f32[128,1,1536]{2,1,0:T(1,128)S(1)} async-done(((f32[128,1,1536]{2,1,0:T(1,128)}), f32[128,1,1536]{2,1,0:T(1,128)S(1)}, u32[]{:S(2)}, u32[]{:S(2)}) %all-to-all-start.1) | async-done | bytes 786464 | tf_op jit(solution)/shard_map/all_to_all | solution.py:161
  66.8 0.6 copy.31
  67.4 1.4 %fusion.13 = f32[32,12,512]{2,0,1:T(8,128)S(1)} fusion(f32[128,12,2,2,32]{0,4,3,2,1:T(8,128)S(1)} %bitcast.89, f32[128,2,2,512,1]{3,0,2,4,1:T(8,128)S(1)} %copy-done.1, s32[32,12]{0,1:T(8,128)S(1)} %copy-done.4, s32[512]{0:T(512)S(1)} %add_abs_fusion), kind=kOutput, calls=%fused_computation.9 | convolution fusion | flops 1208549376 | bytes 2625024 | tf_op jit(solution)/shard_map/dot_general | solution.py:133
  68.9 0.9 copy-done.3
  69.8 2.2 %fusion.32 = bf16[32,12,512]{2,0,1:T(8,128)(2,1)} fusion(f32[32,12,512]{2,0,1:T(8,128)S(1)} %fusion.13, f32[512,512,1]{1,0,2:T(8,128)S(1)} %copy-done.2), kind=kOutput, calls=%fused_computation.16 | convolution fusion | flops 1208352768 | bytes 2228224 | tf_op jit(solution)/shard_map/dot_general | solution.py:113
  72.0 1.7 %copy.33 = bf16[32,12,512]{0,2,1:T(8,128)(2,1)S(1)} copy(bf16[32,12,512]{2,0,1:T(8,128)(2,1)} %fusion.32) | data formatting | bytes 786432 | tf_op jit(solution)/shard_map/convert_element_type | solution.py:120
  73.7 2.5 %copy.34 = bf16[128,12,2,2,32]{0,4,3,2,1:T(8,128)(2,1)} copy(bf16[128,12,2,2,32]{4,3,2,0,1:T(2,128)(2,1)S(1)} %bitcast.85) | data formatting | bytes 786432 | tf_op jit(solution)/shard_map/transpose | solution.py:123
  76.2 2.0 %reduce.3 = bf16[128,1536]{0,1:T(8,128)(2,1)S(1)} reduce(bf16[128,1,1536]{0,2,1:T(8,128)(2,1)} %bitcast.91, bf16[]{:T(256)} %broadcast.38), dimensions={1}, to_apply=%copy.35.reduce_sub_computation | reduce | bytes 786434 | tf_op jit(solution)/shard_map/reshape | solution.py:124
  78.1 0.2 copy.43
  78.3 0.1 reshape.63
  78.4 16.5 %all_to_all.21 = bf16[128,2,768]{2,1,0:T(2,128)(2,1)S(1)} all-to-all(bf16[128,2,768]{2,1,0:T(2,128)(2,1)S(1)} %reshape.63), channel_id=1, replica_groups=mesh['af'=128] {'af'}, dimensions={0} | all-to-all | bytes 786432 | tf_op jit(solution)/shard_map/all_to_all | solution.py:157
  94.9 0.3 reshape.64
  95.3 2.4 %reduce.1 = bf16[128,1536]{1,0:T(8,128)(2,1)S(1)} reduce(bf16[128,1,1536]{2,1,0:T(2,128)(2,1)S(1)} %reshape.64, bf16[]{:T(256)} %constant.19), dimensions={1}, to_apply=%all_to_all.14.reduce_sub_computation | reduce | bytes 786434 | tf_op jit(solution)/shard_map/all_to_all | solution.py:157
  97.6 1.2 reshape.52.y_ref
  98.8 11.0 %shard_map.69 = f32[1536,128]{1,0:T(8,128)} custom-call(bf16[1536,128]{1,0:T(8,128)(2,1)} %reshape.52.y_ref, bf16[2,2,1536,1536]{3,2,1,0:T(8,128)(2,1)} %r_ref.3), custom_call_target="tpu_custom_call" | custom-call | tf_op jit(solution)/shard_map/pallas_call | solution.py:88
  109.8 21.0 %all_to_all.22 = f32[128,1,1536]{2,1,0:T(1,128)S(1)} all-to-all(f32[128,1,1536]{2,1,0:T(1,128)} %bitcast.87), channel_id=1, replica_groups=mesh['af'=128] {'af'}, dimensions={0} | all-to-all | bytes 1572864 | tf_op jit(solution)/shard_map/all_to_all | solution.py:161
  130.8 0.6 copy.37
  131.4 3.5 %fusion.28 = f32[32,12,512]{2,0,1:T(8,128)} fusion(f32[32,12,512]{2,0,1:T(8,128)} %param.7, f32[128,12,2,2,32]{0,4,3,2,1:T(8,128)S(1)} %bitcast.88, f32[128,2,2,512,1]{3,0,2,4,1:T(8,128)S(1)} %copy-done.1, s32[32,12]{0,1:T(8,128)S(1)} %copy-done.4, s32[512]{0:T(512)S(1)} %add_abs_fusion), kind=kOutput, calls=%fused_computation.14 | convolution fusion | flops 1208745984 | bytes 3411456 | tf_op jit(solution)/shard_map/dot_general | solution.py:133
  (9 shorter events, 0.0 us)
Async XLA Ops:
  0.6 1.1 copy-start
  45.9 21.5 %copy-start.1 = (f32[128,2,2,512,1]{3,0,2,4,1:T(8,128)S(1)}, f32[128,2,2,512,1]{3,0,2,4,1:T(8,128)}, u32[]{:S(2)}) copy-start(f32[128,2,2,512,1]{3,0,2,4,1:T(8,128)} %constant.18) | copy-start | bytes 3145732
  45.9 21.5 %copy-start.4 = (s32[32,12]{0,1:T(8,128)S(1)}, s32[32,12]{0,1:T(8,128)}, u32[]{:S(2)}) copy-start(s32[32,12]{0,1:T(8,128)} %param.8) | copy-start | bytes 4612
  45.9 20.9 %all-to-all-start.1 = ((f32[128,1,1536]{2,1,0:T(1,128)}), f32[128,1,1536]{2,1,0:T(1,128)S(1)}, u32[]{:S(2)}, u32[]{:S(2)}) async-start(f32[128,1,1536]{2,1,0:T(1,128)} %bitcast.86), calls=%async_computation.1 | async-start | bytes 1572864 | tf_op jit(solution)/shard_map/all_to_all | solution.py:161
  67.4 2.4 %copy-start.2 = (f32[512,512,1]{1,0,2:T(8,128)S(1)}, f32[512,512,1]{1,0,2:T(8,128)}, u32[]{:S(2)}) copy-start(f32[512,512,1]{1,0,2:T(8,128)} %constant.17) | copy-start | bytes 3145732
  68.9 0.9 copy-start.3

commit v4 on v3

--- a/solution.py
+++ b/solution.py
@@ -121,7 +121,7 @@
     local = table.shape[0] // 2 // groups
     scaled = scaled.reshape(points, stations_dev, groups, local, 2)
     scaled = scaled.transpose(2, 1, 3, 4, 0)
-    return scaled.reshape(groups, 1, stations_dev * local * 2 * points)
+    return scaled.reshape(groups, stations_dev, local * 2 * points)
 
 
 def traces_of(arrived, table, points):
@@ -157,7 +157,7 @@
         arrived = lax.all_to_all(spectra, "af", 0, 0, tiled=True)
         stations = arrived.size // 128
         result = product(reflection, arrived.reshape(stations, 128))
-        result = result.reshape(arrived.shape)
+        result = result.reshape(arrived.shape[0], 1, -1)
         return lax.all_to_all(result, "af", 0, 0, tiled=True)
 
     images = convolve(spectra_of(focus_plus, table, groups), forward_kernel)

time: 135 us -> 130 us (0.963)
  other arithmetic: 7.63 us -> 0.01 us
  blocking collectives: 61 us -> 63.8 us
    all_to_all x2 -> x0, other arithmetic: 4.71 us -> none  [convolve(): arrived = lax.all_to_all(spectra, 'af', 0, 0, tiled=True)]
    reshape x2 -> x0, other arithmetic: 2.92 us -> none  [spectra_of(): return scaled.reshape(groups, 1, stations_dev * local * 2 * points)]
    all_to_all x2, blocking collectives: 40 us -> 42.8 us  [convolve(): arrived = lax.all_to_all(spectra, 'af', 0, 0, tiled=True)]
    unnamed x16 -> x10, local copies, waits for them, and re-layouts: 3.19 us -> 2.02 us
where the time goes in v4:
time: 130 us; the launch traced here: 129 us
  blocking collectives  63.8 us (49%)
  Pallas kernels  21.5 us (17%)
  waiting for transfers between devices  16.3 us (13%)
  local copies, waits for them, and re-layouts  12.6 us (10%)
  matrix products  9.81 us (8%)
  starting transfers between devices  4.55 us (4%)
    all_to_all x2, blocking collectives, convolve(): arrived = lax.all_to_all(spectra, 'af', 0, 0, tiled=True)  42.8 us
    all_to_all x1, blocking collectives, convolve(): return lax.all_to_all(result, 'af', 0, 0, tiled=True)  21 us
    all_to_all x1, waiting for transfers between devices, convolve(): return lax.all_to_all(result, 'af', 0, 0, tiled=True)  16.3 us
    pallas_call x1, Pallas kernels, adjoint_kernel(): pl.pallas_call(_adj_kernel, grid=(stations // TS,), in_specs=[pl.BlockSpe...  11 us
    pallas_call x1, Pallas kernels, forward_kernel(): pl.pallas_call(_fwd_kernel, grid=(stations // TS,), in_specs=[pl.BlockSpe...  10.5 us
    dot_general x2, matrix products, traces_of(): lax.dot_general(spec, tab, (((0, 2, 3), (0, 1, 2)), ((), ())), precision=...  4.93 us
    dot_general x2, matrix products, spectra_of(): lax.dot_general(traces, table, (((2,), (1,)), ((), ())), precision=lax.Pr...  4.88 us
    all_to_all x1, starting transfers between devices, convolve(): return lax.all_to_all(result, 'af', 0, 0, tiled=True)  4.55 us
  transfers between devices with their start and end apart: 1, of which 1 were waited for; matrix products, arithmetic and copies ran while one was open for 0% of the time, Pallas kernels for 0%

profile of v4, /device:TPU:1, one launch (start us, length us, event | category | flops | bytes accessed | tf_op | source)
XLA Modules:
  0.0 129.3 jit_solution(17711312373281037233)
XLA Ops:
  0.6 0.0 copy-start
  0.6 1.1 copy-done
  1.8 2.7 %fusion.33 = bf16[32,12,512]{2,0,1:T(8,128)(2,1)S(1)} fusion(f32[512,512,1]{1,0,2:T(8,128)} %constant.17, f32[32,12,512]{2,0,1:T(8,128)S(1)} %copy-done), kind=kOutput, calls=%fused_computation.17 | convolution fusion | flops 1208352768 | bytes 2228224 | tf_op jit(solution)/shard_map/dot_general | solution.py:113
  4.5 0.8 copy.27
  5.3 0.9 copy.28
  6.2 0.4 copy.29
  6.7 24.8 %all_to_all.20 = bf16[128,12,128]{2,1,0:T(8,128)(2,1)S(1)} all-to-all(bf16[128,12,128]{2,1,0:T(8,128)(2,1)S(1)} %copy.29), channel_id=1, replica_groups=mesh['af'=128] {'af'}, dimensions={0} | all-to-all | bytes 786432 | tf_op jit(solution)/shard_map/all_to_all | solution.py:157
  31.5 0.8 reshape.46.x_ref
  32.3 10.5 %shard_map.68 = f32[1536,128]{1,0:T(8,128)} custom-call(bf16[1536,128]{1,0:T(8,128)(2,1)} %reshape.46.x_ref, bf16[2,2,1536,1536]{3,2,1,0:T(8,128)(2,1)} %r_ref.3), custom_call_target="tpu_custom_call" | custom-call | tf_op jit(solution)/shard_map/pallas_call | solution.py:47
  42.8 0.0 copy-start.1
  42.8 0.0 copy-start.4
  42.8 4.6 %all-to-all-start.1 = ((f32[128,1,1536]{2,1,0:T(1,128)}), f32[128,1,1536]{2,1,0:T(1,128)S(1)}, u32[]{:S(2)}, u32[]{:S(2)}) async-start(f32[128,1,1536]{2,1,0:T(1,128)} %bitcast.86), calls=%async_computation.1 | async-start | bytes 1572864 | tf_op jit(solution)/shard_map/all_to_all | solution.py:161
  47.4 16.3 %all-to-all-done.1 = f32[128,1,1536]{2,1,0:T(1,128)S(1)} async-done(((f32[128,1,1536]{2,1,0:T(1,128)}), f32[128,1,1536]{2,1,0:T(1,128)S(1)}, u32[]{:S(2)}, u32[]{:S(2)}) %all-to-all-start.1) | async-done | bytes 786464 | tf_op jit(solution)/shard_map/all_to_all | solution.py:161
  63.8 0.6 copy.31
  64.3 0.0 copy-start.2
  64.3 0.0 copy-done.1
  64.3 0.0 copy-done.4
  64.4 1.4 %fusion.13 = f32[32,12,512]{2,0,1:T(8,128)S(1)} fusion(f32[128,12,2,2,32]{0,4,3,2,1:T(8,128)S(1)} %bitcast.89, f32[128,2,2,512,1]{3,0,2,4,1:T(8,128)S(1)} %copy-done.1, s32[32,12]{0,1:T(8,128)S(1)} %copy-done.4, s32[512]{0:T(512)S(1)} %add_abs_fusion), kind=kOutput, calls=%fused_computation.9 | convolution fusion | flops 1208549376 | bytes 2625024 | tf_op jit(solution)/shard_map/dot_general | solution.py:133
  65.8 0.0 copy-start.3
  65.8 0.9 copy-done.3
  66.7 0.0 copy-done.2
  66.7 2.2 %fusion.32 = bf16[32,12,512]{2,0,1:T(8,128)(2,1)} fusion(f32[32,12,512]{2,0,1:T(8,128)S(1)} %fusion.13, f32[512,512,1]{1,0,2:T(8,128)S(1)} %copy-done.2), kind=kOutput, calls=%fused_computation.16 | convolution fusion | flops 1208352768 | bytes 2228224 | tf_op jit(solution)/shard_map/dot_general | solution.py:113
  68.9 1.7 %copy.33 = bf16[32,12,512]{0,2,1:T(8,128)(2,1)S(1)} copy(bf16[32,12,512]{2,0,1:T(8,128)(2,1)} %fusion.32) | data formatting | bytes 786432 | tf_op jit(solution)/shard_map/convert_element_type | solution.py:120
  70.6 2.5 %copy.34 = bf16[128,12,2,2,32]{0,4,3,2,1:T(8,128)(2,1)} copy(bf16[128,12,2,2,32]{4,3,2,0,1:T(2,128)(2,1)S(1)} %bitcast.85) | data formatting | bytes 786432 | tf_op jit(solution)/shard_map/transpose | solution.py:123
  73.1 1.4 %copy.35 = bf16[128,12,128]{2,1,0:T(8,128)(2,1)S(1)} copy(bf16[128,12,128]{0,2,1:T(8,128)(2,1)} %bitcast.91) | data formatting | bytes 786432 | tf_op jit(solution)/shard_map/reshape | solution.py:124
  74.5 17.9 %all_to_all.21 = bf16[128,12,128]{2,1,0:T(8,128)(2,1)S(1)} all-to-all(bf16[128,12,128]{2,1,0:T(8,128)(2,1)S(1)} %copy.35), channel_id=1, replica_groups=mesh['af'=128] {'af'}, dimensions={0} | all-to-all | bytes 786432 | tf_op jit(solution)/shard_map/all_to_all | solution.py:157
  92.4 0.8 reshape.52.y_ref
  93.3 11.0 %shard_map.69 = f32[1536,128]{1,0:T(8,128)} custom-call(bf16[1536,128]{1,0:T(8,128)(2,1)} %reshape.52.y_ref, bf16[2,2,1536,1536]{3,2,1,0:T(8,128)(2,1)} %r_ref.3), custom_call_target="tpu_custom_call" | custom-call | tf_op jit(solution)/shard_map/pallas_call | solution.py:88
  104.2 21.0 %all_to_all.22 = f32[128,1,1536]{2,1,0:T(1,128)S(1)} all-to-all(f32[128,1,1536]{2,1,0:T(1,128)} %bitcast.87), channel_id=1, replica_groups=mesh['af'=128] {'af'}, dimensions={0} | all-to-all | bytes 1572864 | tf_op jit(solution)/shard_map/all_to_all | solution.py:161
  125.2 0.6 copy.37
  125.8 3.5 %fusion.28 = f32[32,12,512]{2,0,1:T(8,128)} fusion(f32[32,12,512]{2,0,1:T(8,128)} %param.7, f32[128,12,2,2,32]{0,4,3,2,1:T(8,128)S(1)} %bitcast.88, f32[128,2,2,512,1]{3,0,2,4,1:T(8,128)S(1)} %copy-done.1, s32[32,12]{0,1:T(8,128)S(1)} %copy-done.4, s32[512]{0:T(512)S(1)} %add_abs_fusion), kind=kOutput, calls=%fused_computation.14 | convolution fusion | flops 1208745984 | bytes 3411456 | tf_op jit(solution)/shard_map/dot_general | solution.py:133
  (1 shorter events, 0.0 us)
Async XLA Ops:
  0.6 1.1 copy-start
  42.8 21.5 %copy-start.1 = (f32[128,2,2,512,1]{3,0,2,4,1:T(8,128)S(1)}, f32[128,2,2,512,1]{3,0,2,4,1:T(8,128)}, u32[]{:S(2)}) copy-start(f32[128,2,2,512,1]{3,0,2,4,1:T(8,128)} %constant.18) | copy-start | bytes 3145732
  42.8 21.5 %copy-start.4 = (s32[32,12]{0,1:T(8,128)S(1)}, s32[32,12]{0,1:T(8,128)}, u32[]{:S(2)}) copy-start(s32[32,12]{0,1:T(8,128)} %param.8) | copy-start | bytes 4612
  42.8 20.9 %all-to-all-start.1 = ((f32[128,1,1536]{2,1,0:T(1,128)}), f32[128,1,1536]{2,1,0:T(1,128)S(1)}, u32[]{:S(2)}, u32[]{:S(2)}) async-start(f32[128,1,1536]{2,1,0:T(1,128)} %bitcast.86), calls=%async_computation.1 | async-start | bytes 1572864 | tf_op jit(solution)/shard_map/all_to_all | solution.py:161
  64.3 2.4 %copy-start.2 = (f32[512,512,1]{1,0,2:T(8,128)S(1)}, f32[512,512,1]{1,0,2:T(8,128)}, u32[]{:S(2)}) copy-start(f32[512,512,1]{1,0,2:T(8,128)} %constant.17) | copy-start | bytes 3145732
  65.8 0.9 copy-start.3

commit v5 on v4

--- a/solution.py
+++ b/solution.py
@@ -110,18 +110,13 @@
 
 def spectra_of(traces, table, groups):
     points, stations_dev, ntime = traces.shape
-    mixed = lax.dot_general(
-        traces,
-        table,
-        (((2,), (1,)), ((), ())),
+    tab = table.reshape(groups, table.shape[0] // groups, ntime)
+    mixed = jnp.einsum("pst,dqt->dsqp", traces, tab,
         precision=lax.Precision.HIGHEST,
         preferred_element_type=jnp.float32,
     )
     scaled = (mixed * (1.0 / math.sqrt(ntime))).astype(jnp.bfloat16)
-    local = table.shape[0] // 2 // groups
-    scaled = scaled.reshape(points, stations_dev, groups, local, 2)
-    scaled = scaled.transpose(2, 1, 3, 4, 0)
-    return scaled.reshape(groups, stations_dev, local * 2 * points)
+    return scaled.reshape(groups, stations_dev, tab.shape[1] * points)
 
 
 def traces_of(arrived, table, points):

time: 130 us -> 125 us (0.962)
  local copies, waits for them, and re-layouts: 12.6 us -> 7.05 us
    transpose x2 -> x0, local copies, waits for them, and re-layouts: 3.4 us -> none  [spectra_of(): scaled = scaled.transpose(2, 1, 3, 4, 0)]
    convert_element_type x2 -> x1, local copies, waits for them, and re-layouts: 2.53 us -> 0.03 us  [spectra_of(): scaled = (mixed * (1.0 / math.sqrt(ntime))).astype(jnp.bfloat16)]
where the time goes in v5:
time: 125 us
  blocking collectives  64.1 us (51%)
  Pallas kernels  21.5 us (17%)
  waiting for transfers between devices  16.2 us (13%)
  matrix products  10.8 us (9%)
  local copies, waits for them, and re-layouts  7.05 us (6%)
  starting transfers between devices  4.51 us (4%)
    all_to_all x2, blocking collectives, convolve(): arrived = lax.all_to_all(spectra, 'af', 0, 0, tiled=True)  43.1 us
    all_to_all x1, blocking collectives, convolve(): return lax.all_to_all(result, 'af', 0, 0, tiled=True)  21 us
    all_to_all x1, waiting for transfers between devices, convolve(): return lax.all_to_all(result, 'af', 0, 0, tiled=True)  16.2 us
    pallas_call x1, Pallas kernels, adjoint_kernel(): pl.pallas_call(_adj_kernel, grid=(stations // TS,), in_specs=[pl.BlockSpe...  11 us
    pallas_call x1, Pallas kernels, forward_kernel(): pl.pallas_call(_fwd_kernel, grid=(stations // TS,), in_specs=[pl.BlockSpe...  10.5 us
    dot_general x2, matrix products, spectra_of(): jnp.einsum('pst,dqt->dsqp', traces, tab, precision=lax.Precision.HIGHEST,...  5.64 us
    dot_general x2, matrix products, traces_of(): lax.dot_general(spec, tab, (((0, 2, 3), (0, 1, 2)), ((), ())), precision=...  5.16 us
    all_to_all x1, starting transfers between devices, convolve(): return lax.all_to_all(result, 'af', 0, 0, tiled=True)  4.51 us
  transfers between devices with their start and end apart: 1, of which 1 were waited for; matrix products, arithmetic and copies ran while one was open for 0% of the time, Pallas kernels for 0%

profile of v5, /device:TPU:1, one launch (start us, length us, event | category | flops | bytes accessed | tf_op | source)
XLA Modules:
  0.0 125.0 jit_solution(15721138499374537267)
XLA Ops:
  0.6 0.0 copy-start
  0.6 0.0 copy-start.1
  0.7 0.0 copy-start.3
  0.7 1.1 copy-done
  1.8 2.7 %fusion.33 = bf16[128,12,4,32]{0,3,1,2:T(8,128)(2,1)S(1)} fusion(f32[128,4,512,1]{2,0,3,1:T(8,128)} %constant.18, f32[32,12,512]{2,0,1:T(8,128)S(1)} %copy-done), kind=kOutput, calls=%fused_computation.17 | convolution fusion | flops 1208352768 | bytes 2228224 | tf_op jit(solution)/shard_map/pst,dqt->dsqp/dot_general | solution.py:114
  4.5 0.4 copy.21
  4.9 24.8 %all_to_all.20 = bf16[128,12,128]{2,1,0:T(8,128)(2,1)S(1)} all-to-all(bf16[128,12,128]{2,1,0:T(8,128)(2,1)S(1)} %copy.21), channel_id=1, replica_groups=mesh['af'=128] {'af'}, dimensions={0} | all-to-all | bytes 786432 | tf_op jit(solution)/shard_map/all_to_all | solution.py:152
  29.8 0.8 reshape.44.x_ref
  30.6 10.5 %shard_map.68 = f32[1536,128]{1,0:T(8,128)} custom-call(bf16[1536,128]{1,0:T(8,128)(2,1)} %reshape.44.x_ref, bf16[2,2,1536,1536]{3,2,1,0:T(8,128)(2,1)} %r_ref.3), custom_call_target="tpu_custom_call" | custom-call | tf_op jit(solution)/shard_map/pallas_call | solution.py:47
  41.1 4.5 %all-to-all-start.1 = ((f32[128,1,1536]{2,1,0:T(1,128)}), f32[128,1,1536]{2,1,0:T(1,128)S(1)}, u32[]{:S(2)}, u32[]{:S(2)}) async-start(f32[128,1,1536]{2,1,0:T(1,128)} %bitcast.88), calls=%async_computation.1 | async-start | bytes 1572864 | tf_op jit(solution)/shard_map/all_to_all | solution.py:156
  45.6 16.2 %all-to-all-done.1 = f32[128,1,1536]{2,1,0:T(1,128)S(1)} async-done(((f32[128,1,1536]{2,1,0:T(1,128)}), f32[128,1,1536]{2,1,0:T(1,128)S(1)}, u32[]{:S(2)}, u32[]{:S(2)}) %all-to-all-start.1) | async-done | bytes 786464 | tf_op jit(solution)/shard_map/all_to_all | solution.py:156
  61.9 0.6 copy.23
  62.5 0.0 copy-done.1
  62.5 0.0 copy-done.3
  62.5 1.4 %fusion.13 = f32[32,12,512]{2,0,1:T(8,128)S(1)} fusion(f32[128,12,2,2,32]{0,4,3,2,1:T(8,128)S(1)} %bitcast.91, f32[128,2,2,512,1]{3,0,2,4,1:T(8,128)S(1)} %copy-done.1, s32[32,12]{0,1:T(8,128)S(1)} %copy-done.3, s32[512]{0:T(512)S(1)} %add_abs_fusion), kind=kOutput, calls=%fused_computation.9 | convolution fusion | flops 1208549376 | bytes 2625024 | tf_op jit(solution)/shard_map/dot_general | solution.py:128
  63.9 0.0 copy-start.2
  63.9 3.0 %fusion.32 = bf16[32,12,128,4]{2,0,3,1:T(8,128)(2,1)S(1)} fusion(f32[128,4,512,1]{2,0,1,3:T(8,128)} %constant.20, f32[32,12,512]{2,0,1:T(8,128)S(1)} %fusion.13), kind=kOutput, calls=%fused_computation.16 | convolution fusion | flops 1208352768 | bytes 2228224 | tf_op jit(solution)/shard_map/pst,dqt->dsqp/dot_general | solution.py:114
  66.9 0.4 copy.25
  67.3 18.3 %all_to_all.21 = bf16[128,12,128]{2,1,0:T(8,128)(2,1)} all-to-all(bf16[128,12,128]{2,1,0:T(8,128)(2,1)S(1)} %copy.25), channel_id=1, replica_groups=mesh['af'=128] {'af'}, dimensions={0} | all-to-all | bytes 786432 | tf_op jit(solution)/shard_map/all_to_all | solution.py:152
  85.6 1.9 %reshape.49.y_ref = bf16[1536,128]{1,0:T(8,128)(2,1)} reshape(bf16[128,12,128]{2,1,0:T(8,128)(2,1)} %all_to_all.21) | data formatting | bytes 786432 | tf_op jit(solution)/shard_map/reshape | solution.py:154
  87.5 11.0 %shard_map.69 = f32[1536,128]{1,0:T(8,128)} custom-call(bf16[1536,128]{1,0:T(8,128)(2,1)} %reshape.49.y_ref, bf16[2,2,1536,1536]{3,2,1,0:T(8,128)(2,1)} %r_ref.3), custom_call_target="tpu_custom_call" | custom-call | tf_op jit(solution)/shard_map/pallas_call | solution.py:88
  98.5 21.0 %all_to_all.22 = f32[128,1,1536]{2,1,0:T(1,128)S(1)} all-to-all(f32[128,1,1536]{2,1,0:T(1,128)} %bitcast.89), channel_id=1, replica_groups=mesh['af'=128] {'af'}, dimensions={0} | all-to-all | bytes 1572864 | tf_op jit(solution)/shard_map/all_to_all | solution.py:156
  119.5 1.8 %copy.27 = f32[128,1,1536]{0,2,1:T(8,128)} copy(f32[128,1,1536]{2,1,0:T(1,128)S(1)} %all_to_all.22) | data formatting | bytes 1572864 | tf_op jit(solution)/shard_map/all_to_all | solution.py:156
  121.2 3.7 %fusion.28 = f32[32,12,512]{2,0,1:T(8,128)} fusion(f32[32,12,512]{2,0,1:T(8,128)} %param.7, f32[128,12,2,2,32]{0,4,3,2,1:T(8,128)} %bitcast.90, f32[128,2,2,512,1]{3,0,2,4,1:T(8,128)S(1)} %copy-done.1, s32[32,12]{0,1:T(8,128)S(1)} %copy-done.3, s32[512]{0:T(512)S(1)} %add_abs_fusion), kind=kOutput, calls=%fused_computation.14 | convolution fusion | flops 1208745984 | bytes 3411456 | tf_op jit(solution)/shard_map/dot_general | solution.py:128
  125.0 0.0 copy-done.2
  (2 shorter events, 0.0 us)
Async XLA Ops:
  0.6 1.1 copy-start
  0.6 61.8 %copy-start.1 = (f32[128,2,2,512,1]{3,0,2,4,1:T(8,128)S(1)}, f32[128,2,2,512,1]{3,0,2,4,1:T(8,128)}, u32[]{:S(2)}) copy-start(f32[128,2,2,512,1]{3,0,2,4,1:T(8,128)} %constant.19) | copy-start | bytes 3145732
  0.7 61.8 %copy-start.3 = (s32[32,12]{0,1:T(8,128)S(1)}, s32[32,12]{0,1:T(8,128)}, u32[]{:S(2)}) copy-start(s32[32,12]{0,1:T(8,128)} %param.8) | copy-start | bytes 4612
  41.1 20.8 %all-to-all-start.1 = ((f32[128,1,1536]{2,1,0:T(1,128)}), f32[128,1,1536]{2,1,0:T(1,128)S(1)}, u32[]{:S(2)}, u32[]{:S(2)}) async-start(f32[128,1,1536]{2,1,0:T(1,128)} %bitcast.88), calls=%async_computation.1 | async-start | bytes 1572864 | tf_op jit(solution)/shard_map/all_to_all | solution.py:156
  63.9 61.0 %copy-start.2 = (f32[32,12,512]{2,0,1:T(8,128)}, f32[32,12,512]{2,0,1:T(8,128)S(1)}, u32[]{:S(2)}) copy-start(f32[32,12,512]{2,0,1:T(8,128)S(1)} %fusion.13) | copy-start | bytes 2359300

commit v6 on v5

--- a/solution.py
+++ b/solution.py
@@ -102,10 +102,11 @@
 
 
 def base_table(nfreq, ntime):
-    phase = (np.arange(nfreq)[:, None] * np.arange(ntime)[None, :]) % ntime
-    angle = phase.astype(np.float64) * (2.0 * math.pi / ntime)
-    table = np.stack([np.cos(angle), -np.sin(angle)], 1).reshape(2 * nfreq, ntime)
-    return jnp.asarray(table.astype(np.float32))
+    freq_index = jnp.arange(nfreq, dtype=jnp.int32)
+    time_index = jnp.arange(ntime, dtype=jnp.int32)
+    phase = freq_index[:, None] * time_index[None, :] % ntime
+    angle = phase.astype(jnp.float32) * (2.0 * math.pi / ntime)
+    return jnp.stack([jnp.cos(angle), -jnp.sin(angle)], 1).reshape(2 * nfreq, ntime)
 
 
 def spectra_of(traces, table, groups):

time: 125 us -> 129 us (1.032)
  other arithmetic: 0.01 us -> 4.3 us
  waiting for transfers between devices: 16.2 us -> 13.9 us
  local copies, waits for them, and re-layouts: 7.05 us -> 9.12 us
    all_to_all x2, local copies, waits for them, and re-layouts: 2.32 us -> 4.79 us  [convolve(): return lax.all_to_all(result, 'af', 0, 0, tiled=True)]
    all_to_all x1, waiting for transfers between devices: 16.2 us -> 13.9 us  [convolve(): return lax.all_to_all(result, 'af', 0, 0, tiled=True)]
    cos x0 -> x1, other arithmetic: none -> 2.15 us  [base_table(): jnp.cos(angle)]
    dot_general x2, matrix products: 5.64 us -> 3.52 us  [spectra_of(): jnp.einsum('pst,dqt->dsqp', traces, tab, precision=lax.Precision.HIGHEST,...]
    neg x0 -> x1, other arithmetic: none -> 2.07 us  [base_table(): -jnp.sin(angle)]
    another operation x0 -> x2, local copies, waits for them, and re-layouts: none -> 1.71 us  [the longest x1 0.9 us: spectra_of(): tab = table.reshape(groups, table.shape[0] // groups, ntime)]
  transfers between devices with their start and end apart: 1 -> 1, of which waited for: 1 -> 1; matrix products, arithmetic and copies ran while one was open for 0% -> 2% of each run, Pallas kernels for 0% -> 0%
where the time goes in v6:
time: 129 us
  blocking collectives  63.8 us (49%)
  Pallas kernels  21.5 us (17%)
  waiting for transfers between devices  13.9 us (11%)
  matrix products  9.81 us (8%)
  local copies, waits for them, and re-layouts  9.12 us (7%)
  starting transfers between devices  5.44 us (4%)
  other arithmetic  4.3 us (3%)
    all_to_all x2, blocking collectives, convolve(): arrived = lax.all_to_all(spectra, 'af', 0, 0, tiled=True)  42.8 us
    all_to_all x1, blocking collectives, convolve(): return lax.all_to_all(result, 'af', 0, 0, tiled=True)  21 us
    all_to_all x1, waiting for transfers between devices, convolve(): return lax.all_to_all(result, 'af', 0, 0, tiled=True)  13.9 us
    pallas_call x1, Pallas kernels, adjoint_kernel(): pl.pallas_call(_adj_kernel, grid=(stations // TS,), in_specs=[pl.BlockSpe...  11 us
    pallas_call x1, Pallas kernels, forward_kernel(): pl.pallas_call(_fwd_kernel, grid=(stations // TS,), in_specs=[pl.BlockSpe...  10.5 us
    dot_general x2, matrix products, traces_of(): lax.dot_general(spec, tab, (((0, 2, 3), (0, 1, 2)), ((), ())), precision=...  6.29 us
    all_to_all x1, starting transfers between devices, convolve(): return lax.all_to_all(result, 'af', 0, 0, tiled=True)  5.44 us
    all_to_all x2, local copies, waits for them, and re-layouts, convolve(): return lax.all_to_all(result, 'af', 0, 0, tiled=True)  4.79 us
  transfers between devices with their start and end apart: 1, of which 1 were waited for; matrix products, arithmetic and copies ran while one was open for 2% of the time, Pallas kernels for 0%

profile of v6, /device:TPU:1, one launch (start us, length us, event | category | flops | bytes accessed | tf_op | source)
XLA Modules:
  0.0 128.5 jit_solution(3344640992496870795)
XLA Ops:
  0.6 0.0 copy-start
  0.6 0.0 copy-start.2
  0.7 2.1 %sine_negate_fusion.1 = (f32[256,1,512]{2,0,1:T(8,128)S(1)}, f32[256,1,512]{2,0,1:T(8,128)S(1)}) fusion(), kind=kLoop, calls=%fused_computation.38 | loop fusion | flops 1966080 | bytes 1048576 | tf_op jit(solution)/shard_map/neg | solution.py:109
  2.7 0.1 pad_maximum_fusion
  2.8 0.8 copy.36
  3.6 0.9 reshape_reshape.2
  4.5 0.0 copy-done
  4.5 1.8 %fusion.10 = bf16[128,12,4,32]{0,3,1,2:T(8,128)(2,1)S(1)} fusion(f32[128,4,512,1]{2,1,0,3:T(4,128)S(1)} %bitcast.66, f32[32,12,512]{2,0,1:T(8,128)S(1)} %copy-done), kind=kOutput, calls=%fused_computation.14 | convolution fusion | flops 1208352768 | bytes 2228224 | tf_op jit(solution)/shard_map/pst,dqt->dsqp/dot_general | solution.py:115
  6.3 0.4 copy.39
  6.8 24.8 %all_to_all.20 = bf16[128,12,128]{2,1,0:T(8,128)(2,1)S(1)} all-to-all(bf16[128,12,128]{2,1,0:T(8,128)(2,1)S(1)} %copy.39), channel_id=1, replica_groups=mesh['af'=128] {'af'}, dimensions={0} | all-to-all | bytes 786432 | tf_op jit(solution)/shard_map/all_to_all | solution.py:153
  31.6 0.8 reshape.176.x_ref
  32.5 10.5 %shard_map.59 = f32[1536,128]{1,0:T(8,128)} custom-call(bf16[1536,128]{1,0:T(8,128)(2,1)} %reshape.176.x_ref, bf16[2,2,1536,1536]{3,2,1,0:T(8,128)(2,1)} %r_ref.3), custom_call_target="tpu_custom_call" | custom-call | tf_op jit(solution)/shard_map/pallas_call | solution.py:47
  43.0 5.4 %all-to-all-start.1 = ((f32[128,1,1536]{2,1,0:T(1,128)}), f32[128,1,1536]{2,1,0:T(1,128)}, u32[]{:S(2)}, u32[]{:S(2)}) async-start(f32[128,1,1536]{2,1,0:T(1,128)} %bitcast.68), calls=%async_computation.1 | async-start | bytes 1572864 | tf_op jit(solution)/shard_map/all_to_all | solution.py:157
  48.4 2.1 %fusion.29 = (f32[128,2,1,512]{3,0,2,1:T(8,128)S(1)}, f32[128,2,1,512]{3,0,2,1:T(8,128)S(1)}) fusion(s32[128,2]{0,1:T(2,128)S(1)} %multiply_add_fusion), kind=kLoop, calls=%fused_computation.43 | loop fusion | flops 1966080 | bytes 1049600 | tf_op jit(solution)/shard_map/cos | solution.py:109
  50.6 13.9 %all-to-all-done.1 = f32[128,1,1536]{2,1,0:T(1,128)} async-done(((f32[128,1,1536]{2,1,0:T(1,128)}), f32[128,1,1536]{2,1,0:T(1,128)}, u32[]{:S(2)}, u32[]{:S(2)}) %all-to-all-start.1) | async-done | bytes 786464 | tf_op jit(solution)/shard_map/all_to_all | solution.py:157
  64.4 3.0 %copy.41 = f32[128,1,1536]{0,2,1:T(8,128)} copy(f32[128,1,1536]{2,1,0:T(1,128)} %all-to-all-done.1) | data formatting | bytes 1572864 | tf_op jit(solution)/shard_map/all_to_all | solution.py:157
  67.5 0.0 copy-done.2
  67.5 2.6 %fusion.6 = f32[32,12,512]{2,0,1:T(8,128)S(1)} fusion(f32[128,12,2,2,32]{0,4,3,2,1:T(8,128)} %bitcast.71, f32[128,2,1,512]{3,0,2,1:T(8,128)S(1)} %get-tuple-element.3, f32[128,2,1,512]{3,0,2,1:T(8,128)S(1)} %get-tuple-element.2, s32[32,12]{0,1:T(8,128)S(1)} %copy-done.2, s32[512]{0:T(512)S(1)} %add_abs_fusion), kind=kOutput, calls=%fused_computation.10 | convolution fusion | flops 1208811520 | bytes 2625024 | tf_op jit(solution)/shard_map/dot_general | solution.py:129
  70.0 0.0 copy-start.1
  70.0 1.8 %fusion.9 = bf16[128,12,4,32]{0,3,1,2:T(8,128)(2,1)S(1)} fusion(f32[128,4,512,1]{2,1,0,3:T(4,128)S(1)} %bitcast.67, f32[32,12,512]{2,0,1:T(8,128)S(1)} %fusion.6), kind=kOutput, calls=%fused_computation.13 | convolution fusion | flops 1208352768 | bytes 2228224 | tf_op jit(solution)/shard_map/pst,dqt->dsqp/dot_general | solution.py:115
  71.8 0.0 copy-done.1
  71.9 0.4 copy.45
  72.3 17.9 %all_to_all.21 = bf16[128,12,128]{2,1,0:T(8,128)(2,1)S(1)} all-to-all(bf16[128,12,128]{2,1,0:T(8,128)(2,1)S(1)} %copy.45), channel_id=1, replica_groups=mesh['af'=128] {'af'}, dimensions={0} | all-to-all | bytes 786432 | tf_op jit(solution)/shard_map/all_to_all | solution.py:153
  90.2 0.8 reshape.180.y_ref
  91.1 11.0 %shard_map.60 = f32[1536,128]{1,0:T(8,128)} custom-call(bf16[1536,128]{1,0:T(8,128)(2,1)} %reshape.180.y_ref, bf16[2,2,1536,1536]{3,2,1,0:T(8,128)(2,1)} %r_ref.3), custom_call_target="tpu_custom_call" | custom-call | tf_op jit(solution)/shard_map/pallas_call | solution.py:88
  102.0 21.0 %all_to_all.22 = f32[128,1,1536]{2,1,0:T(1,128)S(1)} all-to-all(f32[128,1,1536]{2,1,0:T(1,128)} %bitcast.69), channel_id=1, replica_groups=mesh['af'=128] {'af'}, dimensions={0} | all-to-all | bytes 1572864 | tf_op jit(solution)/shard_map/all_to_all | solution.py:157
  123.0 1.8 %copy.47 = f32[128,1,1536]{0,2,1:T(8,128)} copy(f32[128,1,1536]{2,1,0:T(1,128)S(1)} %all_to_all.22) | data formatting | bytes 1572864 | tf_op jit(solution)/shard_map/all_to_all | solution.py:157
  124.8 3.7 %fusion.3 = f32[32,12,512]{2,0,1:T(8,128)} fusion(f32[32,12,512]{2,0,1:T(8,128)} %param.6, f32[128,12,2,2,32]{0,4,3,2,1:T(8,128)} %bitcast.70, f32[128,2,1,512]{3,0,2,1:T(8,128)S(1)} %get-tuple-element.3, f32[128,2,1,512]{3,0,2,1:T(8,128)S(1)} %get-tuple-element.2, s32[32,12]{0,1:T(8,128)S(1)} %copy-done.2, s32[512]{0:T(512)S(1)} %add_abs_fusion), kind=kOutput, calls=%fused_computation.6 | convolution fusion | flops 1209008128 | bytes 3411456 | tf_op jit(solution)/shard_map/dot_general | solution.py:129
  (4 shorter events, 0.1 us)
Async XLA Ops:
  0.6 3.9 %copy-start = (f32[32,12,512]{2,0,1:T(8,128)S(1)}, f32[32,12,512]{2,0,1:T(8,128)}, u32[]{:S(2)}) copy-start(f32[32,12,512]{2,0,1:T(8,128)} %param.5) | copy-start | bytes 2359300
  0.6 66.8 %copy-start.2 = (s32[32,12]{0,1:T(8,128)S(1)}, s32[32,12]{0,1:T(8,128)}, u32[]{:S(2)}) copy-start(s32[32,12]{0,1:T(8,128)} %param.7) | copy-start | bytes 4612
  43.0 21.5 %all-to-all-start.1 = ((f32[128,1,1536]{2,1,0:T(1,128)}), f32[128,1,1536]{2,1,0:T(1,128)}, u32[]{:S(2)}, u32[]{:S(2)}) async-start(f32[128,1,1536]{2,1,0:T(1,128)} %bitcast.68), calls=%async_computation.1 | async-start | bytes 1572864 | tf_op jit(solution)/shard_map/all_to_all | solution.py:157
  70.0 1.8 %copy-start.1 = (f32[32,12,512]{2,0,1:T(8,128)}, f32[32,12,512]{2,0,1:T(8,128)S(1)}, u32[]{:S(2)}) copy-start(f32[32,12,512]{2,0,1:T(8,128)S(1)} %fusion.6) | copy-start | bytes 2359300

commit v7 on v5

--- a/solution.py
+++ b/solution.py
@@ -112,7 +112,7 @@
     points, stations_dev, ntime = traces.shape
     tab = table.reshape(groups, table.shape[0] // groups, ntime)
     mixed = jnp.einsum("pst,dqt->dsqp", traces, tab,
-        precision=lax.Precision.HIGHEST,
+        precision=lax.Precision.HIGH,
         preferred_element_type=jnp.float32,
     )
     scaled = (mixed * (1.0 / math.sqrt(ntime))).astype(jnp.bfloat16)
@@ -129,7 +129,7 @@
         spec,
         tab,
         (((0, 2, 3), (0, 1, 2)), ((), ())),
-        precision=lax.Precision.HIGHEST,
+        precision=lax.Precision.HIGH,
         preferred_element_type=jnp.float32,
     )
     scaled = mixed * (1.0 / math.sqrt(table.shape[0] // 2))

time: 125 us -> 123 us (0.984)
  matrix products: 10.8 us -> 8.29 us
    dot_general x2, matrix products: 5.64 us -> 4.38 us  [spectra_of(): jnp.einsum('pst,dqt->dsqp', traces, tab, precision=lax.Precision.HIGH, pr...]
where the time goes in v7:
time: 123 us; the launch traced here: 122 us
  blocking collectives  64.1 us (52%)
  Pallas kernels  21.5 us (17%)
  waiting for transfers between devices  16.2 us (13%)
  matrix products  8.29 us (7%)
  local copies, waits for them, and re-layouts  7.05 us (6%)
  starting transfers between devices  4.51 us (4%)
    all_to_all x2, blocking collectives, convolve(): arrived = lax.all_to_all(spectra, 'af', 0, 0, tiled=True)  43.1 us
    all_to_all x1, blocking collectives, convolve(): return lax.all_to_all(result, 'af', 0, 0, tiled=True)  21 us
    all_to_all x1, waiting for transfers between devices, convolve(): return lax.all_to_all(result, 'af', 0, 0, tiled=True)  16.2 us
    pallas_call x1, Pallas kernels, adjoint_kernel(): pl.pallas_call(_adj_kernel, grid=(stations // TS,), in_specs=[pl.BlockSpe...  11 us
    pallas_call x1, Pallas kernels, forward_kernel(): pl.pallas_call(_fwd_kernel, grid=(stations // TS,), in_specs=[pl.BlockSpe...  10.5 us
    all_to_all x1, starting transfers between devices, convolve(): return lax.all_to_all(result, 'af', 0, 0, tiled=True)  4.51 us
    dot_general x2, matrix products, spectra_of(): jnp.einsum('pst,dqt->dsqp', traces, tab, precision=lax.Precision.HIGH, pr...  4.38 us
    dot_general x2, matrix products, traces_of(): lax.dot_general(spec, tab, (((0, 2, 3), (0, 1, 2)), ((), ())), precision=...  3.91 us
  transfers between devices with their start and end apart: 1, of which 1 were waited for; matrix products, arithmetic and copies ran while one was open for 0% of the time, Pallas kernels for 0%

profile of v7, /device:TPU:1, one launch (start us, length us, event | category | flops | bytes accessed | tf_op | source)
XLA Modules:
  0.0 122.4 jit_solution(4744112328406953866)
XLA Ops:
  0.6 0.0 copy-start
  0.6 0.0 copy-start.1
  0.7 0.0 copy-start.3
  0.7 1.1 copy-done
  1.8 2.0 %fusion.33 = bf16[128,12,4,32]{0,3,1,2:T(8,128)(2,1)S(1)} fusion(f32[128,4,512,1]{2,0,3,1:T(8,128)} %constant.18, f32[32,12,512]{2,0,1:T(8,128)S(1)} %copy-done), kind=kOutput, calls=%fused_computation.17 | convolution fusion | flops 604372992 | bytes 2228224 | tf_op jit(solution)/shard_map/pst,dqt->dsqp/dot_general | solution.py:114
  3.9 0.4 copy.21
  4.3 24.8 %all_to_all.20 = bf16[128,12,128]{2,1,0:T(8,128)(2,1)S(1)} all-to-all(bf16[128,12,128]{2,1,0:T(8,128)(2,1)S(1)} %copy.21), channel_id=1, replica_groups=mesh['af'=128] {'af'}, dimensions={0} | all-to-all | bytes 786432 | tf_op jit(solution)/shard_map/all_to_all | solution.py:152
  29.1 0.8 reshape.44.x_ref
  30.0 10.5 %shard_map.68 = f32[1536,128]{1,0:T(8,128)} custom-call(bf16[1536,128]{1,0:T(8,128)(2,1)} %reshape.44.x_ref, bf16[2,2,1536,1536]{3,2,1,0:T(8,128)(2,1)} %r_ref.3), custom_call_target="tpu_custom_call" | custom-call | tf_op jit(solution)/shard_map/pallas_call | solution.py:47
  40.5 4.5 %all-to-all-start.1 = ((f32[128,1,1536]{2,1,0:T(1,128)}), f32[128,1,1536]{2,1,0:T(1,128)S(1)}, u32[]{:S(2)}, u32[]{:S(2)}) async-start(f32[128,1,1536]{2,1,0:T(1,128)} %bitcast.88), calls=%async_computation.1 | async-start | bytes 1572864 | tf_op jit(solution)/shard_map/all_to_all | solution.py:156
  45.0 16.2 %all-to-all-done.1 = f32[128,1,1536]{2,1,0:T(1,128)S(1)} async-done(((f32[128,1,1536]{2,1,0:T(1,128)}), f32[128,1,1536]{2,1,0:T(1,128)S(1)}, u32[]{:S(2)}, u32[]{:S(2)}) %all-to-all-start.1) | async-done | bytes 786464 | tf_op jit(solution)/shard_map/all_to_all | solution.py:156
  61.2 0.6 copy.23
  61.8 0.0 copy-done.1
  61.8 0.0 copy-done.3
  61.8 0.8 fusion.13
  62.7 0.0 copy-start.2
  62.7 2.3 %fusion.32 = bf16[32,12,128,4]{2,0,3,1:T(8,128)(2,1)S(1)} fusion(f32[128,4,512,1]{2,0,1,3:T(8,128)} %constant.20, f32[32,12,512]{2,0,1:T(8,128)S(1)} %fusion.13), kind=kOutput, calls=%fused_computation.16 | convolution fusion | flops 604372992 | bytes 2228224 | tf_op jit(solution)/shard_map/pst,dqt->dsqp/dot_general | solution.py:114
  65.0 0.4 copy.25
  65.4 18.3 %all_to_all.21 = bf16[128,12,128]{2,1,0:T(8,128)(2,1)} all-to-all(bf16[128,12,128]{2,1,0:T(8,128)(2,1)S(1)} %copy.25), channel_id=1, replica_groups=mesh['af'=128] {'af'}, dimensions={0} | all-to-all | bytes 786432 | tf_op jit(solution)/shard_map/all_to_all | solution.py:152
  83.7 1.9 %reshape.49.y_ref = bf16[1536,128]{1,0:T(8,128)(2,1)} reshape(bf16[128,12,128]{2,1,0:T(8,128)(2,1)} %all_to_all.21) | data formatting | bytes 786432 | tf_op jit(solution)/shard_map/reshape | solution.py:154
  85.6 11.0 %shard_map.69 = f32[1536,128]{1,0:T(8,128)} custom-call(bf16[1536,128]{1,0:T(8,128)(2,1)} %reshape.49.y_ref, bf16[2,2,1536,1536]{3,2,1,0:T(8,128)(2,1)} %r_ref.3), custom_call_target="tpu_custom_call" | custom-call | tf_op jit(solution)/shard_map/pallas_call | solution.py:88
  96.6 21.0 %all_to_all.22 = f32[128,1,1536]{2,1,0:T(1,128)S(1)} all-to-all(f32[128,1,1536]{2,1,0:T(1,128)} %bitcast.89), channel_id=1, replica_groups=mesh['af'=128] {'af'}, dimensions={0} | all-to-all | bytes 1572864 | tf_op jit(solution)/shard_map/all_to_all | solution.py:156
  117.6 1.8 %copy.27 = f32[128,1,1536]{0,2,1:T(8,128)} copy(f32[128,1,1536]{2,1,0:T(1,128)S(1)} %all_to_all.22) | data formatting | bytes 1572864 | tf_op jit(solution)/shard_map/all_to_all | solution.py:156
  119.3 3.1 %fusion.28 = f32[32,12,512]{2,0,1:T(8,128)} fusion(f32[32,12,512]{2,0,1:T(8,128)} %param.7, f32[128,12,2,2,32]{0,4,3,2,1:T(8,128)} %bitcast.90, f32[128,2,2,512,1]{3,0,2,4,1:T(8,128)S(1)} %copy-done.1, s32[32,12]{0,1:T(8,128)S(1)} %copy-done.3, s32[512]{0:T(512)S(1)} %add_abs_fusion), kind=kOutput, calls=%fused_computation.14 | convolution fusion | flops 604766208 | bytes 3411456 | tf_op jit(solution)/shard_map/dot_general | solution.py:128
  122.4 0.0 copy-done.2
  (2 shorter events, 0.0 us)
Async XLA Ops:
  0.6 1.1 copy-start
  0.6 61.2 %copy-start.1 = (f32[128,2,2,512,1]{3,0,2,4,1:T(8,128)S(1)}, f32[128,2,2,512,1]{3,0,2,4,1:T(8,128)}, u32[]{:S(2)}) copy-start(f32[128,2,2,512,1]{3,0,2,4,1:T(8,128)} %constant.19) | copy-start | bytes 3145732
  0.7 61.2 %copy-start.3 = (s32[32,12]{0,1:T(8,128)S(1)}, s32[32,12]{0,1:T(8,128)}, u32[]{:S(2)}) copy-start(s32[32,12]{0,1:T(8,128)} %param.8) | copy-start | bytes 4612
  40.5 20.8 %all-to-all-start.1 = ((f32[128,1,1536]{2,1,0:T(1,128)}), f32[128,1,1536]{2,1,0:T(1,128)S(1)}, u32[]{:S(2)}, u32[]{:S(2)}) async-start(f32[128,1,1536]{2,1,0:T(1,128)} %bitcast.88), calls=%async_computation.1 | async-start | bytes 1572864 | tf_op jit(solution)/shard_map/all_to_all | solution.py:156
  62.7 59.8 %copy-start.2 = (f32[32,12,512]{2,0,1:T(8,128)}, f32[32,12,512]{2,0,1:T(8,128)S(1)}, u32[]{:S(2)}) copy-start(f32[32,12,512]{2,0,1:T(8,128)S(1)} %fusion.13) | copy-start | bytes 2359300

commit v8 on v7

--- a/solution.py
+++ b/solution.py
@@ -12,6 +12,7 @@
 NFREQ = 256
 NT = 512
 TS = 512
+TS_ADJ = 768
 
 
 def _partner(x, negate_first):
@@ -65,9 +66,9 @@
         yp_ref[...] = _partner(y_ref[...], False)
         acc_ref[...] = jnp.zeros(acc_ref.shape, jnp.float32)
 
-    off = pl.multiple_of(i * TS, TS)
-    y = y_ref[pl.ds(off, TS), :]
-    yp = yp_ref[pl.ds(off, TS), :]
+    off = pl.multiple_of(i * TS_ADJ, TS_ADJ)
+    y = y_ref[pl.ds(off, TS_ADJ), :]
+    yp = yp_ref[pl.ds(off, TS_ADJ), :]
     dims = (((0,), (0,)), ((), ()))
     parts = []
     for kl in range(2):
@@ -87,10 +88,10 @@
     stations = y.shape[0]
     return pl.pallas_call(
         _adj_kernel,
-        grid=(stations // TS,),
+        grid=(stations // TS_ADJ,),
         in_specs=[
             pl.BlockSpec((stations, 128), lambda i: (0, 0)),
-            pl.BlockSpec((2, 2, TS, stations), lambda i: (0, 0, i, 0)),
+            pl.BlockSpec((2, 2, TS_ADJ, stations), lambda i: (0, 0, i, 0)),
         ],
         out_specs=pl.BlockSpec((stations, 128), lambda i: (0, 0)),
         out_shape=jax.ShapeDtypeStruct((stations, 128), jnp.float32),

time: 123 us -> 123 us (level)
  no operation moved by 1% of the time
where the time goes in v8:
time: 123 us; the launch traced here: 122 us
  blocking collectives  64.1 us (52%)
  Pallas kernels  21.4 us (17%)
  waiting for transfers between devices  16.2 us (13%)
  matrix products  8.29 us (7%)
  local copies, waits for them, and re-layouts  7.05 us (6%)
  starting transfers between devices  4.51 us (4%)
    all_to_all x2, blocking collectives, convolve(): arrived = lax.all_to_all(spectra, 'af', 0, 0, tiled=True)  43.1 us
    all_to_all x1, blocking collectives, convolve(): return lax.all_to_all(result, 'af', 0, 0, tiled=True)  21 us
    all_to_all x1, waiting for transfers between devices, convolve(): return lax.all_to_all(result, 'af', 0, 0, tiled=True)  16.2 us
    pallas_call x1, Pallas kernels, adjoint_kernel(): pl.pallas_call(_adj_kernel, grid=(stations // TS_ADJ,), in_specs=[pl.Bloc...  10.9 us
    pallas_call x1, Pallas kernels, forward_kernel(): pl.pallas_call(_fwd_kernel, grid=(stations // TS,), in_specs=[pl.BlockSpe...  10.5 us
    all_to_all x1, starting transfers between devices, convolve(): return lax.all_to_all(result, 'af', 0, 0, tiled=True)  4.51 us
    dot_general x2, matrix products, spectra_of(): jnp.einsum('pst,dqt->dsqp', traces, tab, precision=lax.Precision.HIGH, pr...  4.38 us
    dot_general x2, matrix products, traces_of(): lax.dot_general(spec, tab, (((0, 2, 3), (0, 1, 2)), ((), ())), precision=...  3.92 us
  transfers between devices with their start and end apart: 1, of which 1 were waited for; matrix products, arithmetic and copies ran while one was open for 0% of the time, Pallas kernels for 0%

profile of v8, /device:TPU:1, one launch (start us, length us, event | category | flops | bytes accessed | tf_op | source)
XLA Modules:
  0.0 122.3 jit_solution(2532599436572892500)
XLA Ops:
  0.6 0.0 copy-start
  0.6 0.0 copy-start.1
  0.7 0.0 copy-start.3
  0.7 1.1 copy-done
  1.8 2.0 %fusion.33 = bf16[128,12,4,32]{0,3,1,2:T(8,128)(2,1)S(1)} fusion(f32[128,4,512,1]{2,0,3,1:T(8,128)} %constant.18, f32[32,12,512]{2,0,1:T(8,128)S(1)} %copy-done), kind=kOutput, calls=%fused_computation.17 | convolution fusion | flops 604372992 | bytes 2228224 | tf_op jit(solution)/shard_map/pst,dqt->dsqp/dot_general | solution.py:115
  3.9 0.4 copy.21
  4.3 24.8 %all_to_all.20 = bf16[128,12,128]{2,1,0:T(8,128)(2,1)S(1)} all-to-all(bf16[128,12,128]{2,1,0:T(8,128)(2,1)S(1)} %copy.21), channel_id=1, replica_groups=mesh['af'=128] {'af'}, dimensions={0} | all-to-all | bytes 786432 | tf_op jit(solution)/shard_map/all_to_all | solution.py:153
  29.1 0.8 reshape.44.x_ref
  30.0 10.5 %shard_map.68 = f32[1536,128]{1,0:T(8,128)} custom-call(bf16[1536,128]{1,0:T(8,128)(2,1)} %reshape.44.x_ref, bf16[2,2,1536,1536]{3,2,1,0:T(8,128)(2,1)} %r_ref.3), custom_call_target="tpu_custom_call" | custom-call | tf_op jit(solution)/shard_map/pallas_call | solution.py:48
  40.5 4.5 %all-to-all-start.1 = ((f32[128,1,1536]{2,1,0:T(1,128)}), f32[128,1,1536]{2,1,0:T(1,128)S(1)}, u32[]{:S(2)}, u32[]{:S(2)}) async-start(f32[128,1,1536]{2,1,0:T(1,128)} %bitcast.88), calls=%async_computation.1 | async-start | bytes 1572864 | tf_op jit(solution)/shard_map/all_to_all | solution.py:157
  45.0 16.2 %all-to-all-done.1 = f32[128,1,1536]{2,1,0:T(1,128)S(1)} async-done(((f32[128,1,1536]{2,1,0:T(1,128)}), f32[128,1,1536]{2,1,0:T(1,128)S(1)}, u32[]{:S(2)}, u32[]{:S(2)}) %all-to-all-start.1) | async-done | bytes 786464 | tf_op jit(solution)/shard_map/all_to_all | solution.py:157
  61.2 0.6 copy.23
  61.8 0.0 copy-done.1
  61.8 0.0 copy-done.3
  61.8 0.8 fusion.13
  62.7 0.0 copy-start.2
  62.7 2.3 %fusion.32 = bf16[32,12,128,4]{2,0,3,1:T(8,128)(2,1)S(1)} fusion(f32[128,4,512,1]{2,0,1,3:T(8,128)} %constant.20, f32[32,12,512]{2,0,1:T(8,128)S(1)} %fusion.13), kind=kOutput, calls=%fused_computation.16 | convolution fusion | flops 604372992 | bytes 2228224 | tf_op jit(solution)/shard_map/pst,dqt->dsqp/dot_general | solution.py:115
  65.0 0.4 copy.25
  65.4 18.3 %all_to_all.21 = bf16[128,12,128]{2,1,0:T(8,128)(2,1)} all-to-all(bf16[128,12,128]{2,1,0:T(8,128)(2,1)S(1)} %copy.25), channel_id=1, replica_groups=mesh['af'=128] {'af'}, dimensions={0} | all-to-all | bytes 786432 | tf_op jit(solution)/shard_map/all_to_all | solution.py:153
  83.7 1.9 %reshape.49.y_ref = bf16[1536,128]{1,0:T(8,128)(2,1)} reshape(bf16[128,12,128]{2,1,0:T(8,128)(2,1)} %all_to_all.21) | data formatting | bytes 786432 | tf_op jit(solution)/shard_map/reshape | solution.py:155
  85.6 10.9 %shard_map.69 = f32[1536,128]{1,0:T(8,128)} custom-call(bf16[1536,128]{1,0:T(8,128)(2,1)} %reshape.49.y_ref, bf16[2,2,1536,1536]{3,2,1,0:T(8,128)(2,1)} %r_ref.3), custom_call_target="tpu_custom_call" | custom-call | tf_op jit(solution)/shard_map/pallas_call | solution.py:89
  96.5 21.0 %all_to_all.22 = f32[128,1,1536]{2,1,0:T(1,128)S(1)} all-to-all(f32[128,1,1536]{2,1,0:T(1,128)} %bitcast.89), channel_id=1, replica_groups=mesh['af'=128] {'af'}, dimensions={0} | all-to-all | bytes 1572864 | tf_op jit(solution)/shard_map/all_to_all | solution.py:157
  117.5 1.8 %copy.27 = f32[128,1,1536]{0,2,1:T(8,128)} copy(f32[128,1,1536]{2,1,0:T(1,128)S(1)} %all_to_all.22) | data formatting | bytes 1572864 | tf_op jit(solution)/shard_map/all_to_all | solution.py:157
  119.2 3.1 %fusion.28 = f32[32,12,512]{2,0,1:T(8,128)} fusion(f32[32,12,512]{2,0,1:T(8,128)} %param.7, f32[128,12,2,2,32]{0,4,3,2,1:T(8,128)} %bitcast.90, f32[128,2,2,512,1]{3,0,2,4,1:T(8,128)S(1)} %copy-done.1, s32[32,12]{0,1:T(8,128)S(1)} %copy-done.3, s32[512]{0:T(512)S(1)} %add_abs_fusion), kind=kOutput, calls=%fused_computation.14 | convolution fusion | flops 604766208 | bytes 3411456 | tf_op jit(solution)/shard_map/dot_general | solution.py:129
  122.3 0.0 copy-done.2
  (2 shorter events, 0.0 us)
Async XLA Ops:
  0.6 1.1 copy-start
  0.6 61.2 %copy-start.1 = (f32[128,2,2,512,1]{3,0,2,4,1:T(8,128)S(1)}, f32[128,2,2,512,1]{3,0,2,4,1:T(8,128)}, u32[]{:S(2)}) copy-start(f32[128,2,2,512,1]{3,0,2,4,1:T(8,128)} %constant.19) | copy-start | bytes 3145732
  0.7 61.2 %copy-start.3 = (s32[32,12]{0,1:T(8,128)S(1)}, s32[32,12]{0,1:T(8,128)}, u32[]{:S(2)}) copy-start(s32[32,12]{0,1:T(8,128)} %param.8) | copy-start | bytes 4612
  40.5 20.8 %all-to-all-start.1 = ((f32[128,1,1536]{2,1,0:T(1,128)}), f32[128,1,1536]{2,1,0:T(1,128)S(1)}, u32[]{:S(2)}, u32[]{:S(2)}) async-start(f32[128,1,1536]{2,1,0:T(1,128)} %bitcast.88), calls=%async_computation.1 | async-start | bytes 1572864 | tf_op jit(solution)/shard_map/all_to_all | solution.py:157
  62.7 59.7 %copy-start.2 = (f32[32,12,512]{2,0,1:T(8,128)}, f32[32,12,512]{2,0,1:T(8,128)S(1)}, u32[]{:S(2)}) copy-start(f32[32,12,512]{2,0,1:T(8,128)S(1)} %fusion.13) | copy-start | bytes 2359300

commit v9 on v7

--- a/solution.py
+++ b/solution.py
@@ -27,9 +27,22 @@
     return out.astype(jnp.bfloat16)
 
 
-def _fwd_kernel(x_ref, r_ref, o_ref, xp_ref):
+def _gather(src_hbm, dst_ref, sems):
+    groups, rows = src_hbm.shape[0], src_hbm.shape[1]
+    copies = [
+        pltpu.make_async_copy(src_hbm.at[j], dst_ref.at[pl.ds(j * rows, rows)], sems.at[j])
+        for j in range(groups)
+    ]
+    for c in copies:
+        c.start()
+    for c in copies:
+        c.wait()
+
+
+def _fwd_kernel(xa_hbm, r_ref, o_ref, x_ref, xp_ref, sems):
     @pl.when(pl.program_id(0) == 0)
     def _():
+        _gather(xa_hbm, x_ref, sems)
         xp_ref[...] = _partner(x_ref[...], True)
 
     parts = []
@@ -43,25 +56,30 @@
 
 
 def forward_kernel(reflection, x):
-    stations = x.shape[0]
+    stations = x.shape[0] * x.shape[1]
     return pl.pallas_call(
         _fwd_kernel,
         grid=(stations // TS,),
         in_specs=[
-            pl.BlockSpec((stations, 128), lambda i: (0, 0)),
+            pl.BlockSpec(memory_space=pl.ANY),
             pl.BlockSpec((2, 2, TS, stations), lambda i: (0, 0, i, 0)),
         ],
         out_specs=pl.BlockSpec((TS, 128), lambda i: (i, 0)),
         out_shape=jax.ShapeDtypeStruct((stations, 128), jnp.float32),
-        scratch_shapes=[pltpu.VMEM((stations, 128), jnp.bfloat16)],
+        scratch_shapes=[
+            pltpu.VMEM((stations, 128), jnp.bfloat16),
+            pltpu.VMEM((stations, 128), jnp.bfloat16),
+            pltpu.SemaphoreType.DMA((x.shape[0],)),
+        ],
     )(x, reflection)
 
 
-def _adj_kernel(y_ref, r_ref, o_ref, yp_ref, acc_ref):
+def _adj_kernel(ya_hbm, r_ref, o_ref, y_ref, yp_ref, acc_ref, sems):
     i = pl.program_id(0)
 
     @pl.when(i == 0)
     def _():
+        _gather(ya_hbm, y_ref, sems)
         yp_ref[...] = _partner(y_ref[...], False)
         acc_ref[...] = jnp.zeros(acc_ref.shape, jnp.float32)
 
@@ -84,19 +102,21 @@
 
 
 def adjoint_kernel(reflection, y):
-    stations = y.shape[0]
+    stations = y.shape[0] * y.shape[1]
     return pl.pallas_call(
         _adj_kernel,
         grid=(stations // TS,),
         in_specs=[
-            pl.BlockSpec((stations, 128), lambda i: (0, 0)),
+            pl.BlockSpec(memory_space=pl.ANY),
             pl.BlockSpec((2, 2, TS, stations), lambda i: (0, 0, i, 0)),
         ],
         out_specs=pl.BlockSpec((stations, 128), lambda i: (0, 0)),
         out_shape=jax.ShapeDtypeStruct((stations, 128), jnp.float32),
         scratch_shapes=[
             pltpu.VMEM((stations, 128), jnp.bfloat16),
+            pltpu.VMEM((stations, 128), jnp.bfloat16),
             pltpu.VMEM((stations, 128), jnp.float32),
+            pltpu.SemaphoreType.DMA((y.shape[0],)),
         ],
     )(y, reflection)
 
@@ -150,8 +170,7 @@
 
     def convolve(spectra, product):
         arrived = lax.all_to_all(spectra, "af", 0, 0, tiled=True)
-        stations = arrived.size // 128
-        result = product(reflection, arrived.reshape(stations, 128))
+        result = product(reflection, arrived)
         result = result.reshape(arrived.shape[0], 1, -1)
         return lax.all_to_all(result, "af", 0, 0, tiled=True)
 

time: 123 us -> 127 us (1.033)
  Pallas kernels: 21.5 us -> 28.1 us
  local copies, waits for them, and re-layouts: 7.05 us -> 4.33 us
    pallas_call x1, Pallas kernels: 10.5 us -> 13.8 us  [forward_kernel(): pl.pallas_call(_fwd_kernel, grid=(stations // TS,), in_specs=[pl.BlockSpe...]
    pallas_call x1, Pallas kernels: 11 us -> 14.3 us  [adjoint_kernel(): pl.pallas_call(_adj_kernel, grid=(stations // TS,), in_specs=[pl.BlockSpe...]
    reshape x2 -> x0, local copies, waits for them, and re-layouts: 2.72 us -> none  [convolve(): result = product(reflection, arrived.reshape(stations, 128))]
where the time goes in v9:
time: 127 us; the launch traced here: 126 us
  blocking collectives  64.2 us (51%)
  Pallas kernels  28.1 us (22%)
  waiting for transfers between devices  16.3 us (13%)
  matrix products  8.29 us (7%)
  starting transfers between devices  4.52 us (4%)
  local copies, waits for them, and re-layouts  4.33 us (3%)
    all_to_all x2, blocking collectives, convolve(): arrived = lax.all_to_all(spectra, 'af', 0, 0, tiled=True)  43.2 us
    all_to_all x1, blocking collectives, convolve(): return lax.all_to_all(result, 'af', 0, 0, tiled=True)  21 us
    all_to_all x1, waiting for transfers between devices, convolve(): return lax.all_to_all(result, 'af', 0, 0, tiled=True)  16.3 us
    pallas_call x1, Pallas kernels, adjoint_kernel(): pl.pallas_call(_adj_kernel, grid=(stations // TS,), in_specs=[pl.BlockSpe...  14.3 us
    pallas_call x1, Pallas kernels, forward_kernel(): pl.pallas_call(_fwd_kernel, grid=(stations // TS,), in_specs=[pl.BlockSpe...  13.8 us
    all_to_all x1, starting transfers between devices, convolve(): return lax.all_to_all(result, 'af', 0, 0, tiled=True)  4.52 us
    dot_general x2, matrix products, spectra_of(): jnp.einsum('pst,dqt->dsqp', traces, tab, precision=lax.Precision.HIGH, pr...  4.37 us
    dot_general x2, matrix products, traces_of(): lax.dot_general(spec, tab, (((0, 2, 3), (0, 1, 2)), ((), ())), precision=...  3.91 us
  transfers between devices with their start and end apart: 1, of which 1 were waited for; matrix products, arithmetic and copies ran while one was open for 0% of the time, Pallas kernels for 0%

profile of v9, /device:TPU:1, one launch (start us, length us, event | category | flops | bytes accessed | tf_op | source)
XLA Modules:
  0.0 126.5 jit_solution(16865136995240713055)
XLA Ops:
  0.6 0.0 copy-start
  0.6 0.0 copy-start.1
  0.7 0.0 copy-start.3
  0.7 1.1 copy-done
  1.8 2.0 %fusion.33 = bf16[128,12,4,32]{0,3,1,2:T(8,128)(2,1)S(1)} fusion(f32[128,4,512,1]{2,0,3,1:T(8,128)} %constant.18, f32[32,12,512]{2,0,1:T(8,128)S(1)} %copy-done), kind=kOutput, calls=%fused_computation.17 | convolution fusion | flops 604372992 | bytes 2228224 | tf_op jit(solution)/shard_map/pst,dqt->dsqp/dot_general | solution.py:134
  3.9 0.4 copy.22
  4.3 24.9 %all_to_all.20.xa_hbm = bf16[128,12,128]{2,1,0:T(8,128)(2,1)} all-to-all(bf16[128,12,128]{2,1,0:T(8,128)(2,1)S(1)} %copy.22), channel_id=1, replica_groups=mesh['af'=128] {'af'}, dimensions={0} | all-to-all | bytes 786432 | tf_op jit(solution)/shard_map/all_to_all | solution.py:172
  29.2 13.8 %shard_map.68 = f32[1536,128]{1,0:T(8,128)} custom-call(bf16[128,12,128]{2,1,0:T(8,128)(2,1)} %all_to_all.20.xa_hbm, bf16[2,2,1536,1536]{3,2,1,0:T(8,128)(2,1)} %r_ref.3), custom_call_target="tpu_custom_call" | custom-call | tf_op jit(solution)/shard_map/pallas_call | solution.py:60
  43.0 4.5 %all-to-all-start.1 = ((f32[128,1,1536]{2,1,0:T(1,128)}), f32[128,1,1536]{2,1,0:T(1,128)S(1)}, u32[]{:S(2)}, u32[]{:S(2)}) async-start(f32[128,1,1536]{2,1,0:T(1,128)} %bitcast.88), calls=%async_computation.1 | async-start | bytes 1572864 | tf_op jit(solution)/shard_map/all_to_all | solution.py:175
  47.6 16.3 %all-to-all-done.1 = f32[128,1,1536]{2,1,0:T(1,128)S(1)} async-done(((f32[128,1,1536]{2,1,0:T(1,128)}), f32[128,1,1536]{2,1,0:T(1,128)S(1)}, u32[]{:S(2)}, u32[]{:S(2)}) %all-to-all-start.1) | async-done | bytes 786464 | tf_op jit(solution)/shard_map/all_to_all | solution.py:175
  63.8 0.6 copy.24
  64.4 0.0 copy-done.1
  64.4 0.0 copy-done.3
  64.4 0.8 fusion.13
  65.2 0.0 copy-start.2
  65.3 2.3 %fusion.32 = bf16[32,12,128,4]{2,0,3,1:T(8,128)(2,1)S(1)} fusion(f32[128,4,512,1]{2,0,1,3:T(8,128)} %constant.20, f32[32,12,512]{2,0,1:T(8,128)S(1)} %fusion.13), kind=kOutput, calls=%fused_computation.16 | convolution fusion | flops 604372992 | bytes 2228224 | tf_op jit(solution)/shard_map/pst,dqt->dsqp/dot_general | solution.py:134
  67.6 0.4 copy.26
  68.0 18.3 %all_to_all.21.ya_hbm = bf16[128,12,128]{2,1,0:T(8,128)(2,1)} all-to-all(bf16[128,12,128]{2,1,0:T(8,128)(2,1)S(1)} %copy.26), channel_id=1, replica_groups=mesh['af'=128] {'af'}, dimensions={0} | all-to-all | bytes 786432 | tf_op jit(solution)/shard_map/all_to_all | solution.py:172
  86.3 14.3 %shard_map.69 = f32[1536,128]{1,0:T(8,128)} custom-call(bf16[128,12,128]{2,1,0:T(8,128)(2,1)} %all_to_all.21.ya_hbm, bf16[2,2,1536,1536]{3,2,1,0:T(8,128)(2,1)} %r_ref.3), custom_call_target="tpu_custom_call" | custom-call | tf_op jit(solution)/shard_map/pallas_call | solution.py:106
  100.6 21.0 %all_to_all.22 = f32[128,1,1536]{2,1,0:T(1,128)S(1)} all-to-all(f32[128,1,1536]{2,1,0:T(1,128)} %bitcast.89), channel_id=1, replica_groups=mesh['af'=128] {'af'}, dimensions={0} | all-to-all | bytes 1572864 | tf_op jit(solution)/shard_map/all_to_all | solution.py:175
  121.6 1.8 %copy.28 = f32[128,1,1536]{0,2,1:T(8,128)} copy(f32[128,1,1536]{2,1,0:T(1,128)S(1)} %all_to_all.22) | data formatting | bytes 1572864 | tf_op jit(solution)/shard_map/all_to_all | solution.py:175
  123.4 3.1 %fusion.28 = f32[32,12,512]{2,0,1:T(8,128)} fusion(f32[32,12,512]{2,0,1:T(8,128)} %param.7, f32[128,12,2,2,32]{0,4,3,2,1:T(8,128)} %bitcast.90, f32[128,2,2,512,1]{3,0,2,4,1:T(8,128)S(1)} %copy-done.1, s32[32,12]{0,1:T(8,128)S(1)} %copy-done.3, s32[512]{0:T(512)S(1)} %add_abs_fusion), kind=kOutput, calls=%fused_computation.14 | convolution fusion | flops 604766208 | bytes 3411456 | tf_op jit(solution)/shard_map/dot_general | solution.py:148
  126.5 0.0 copy-done.2
  (2 shorter events, 0.0 us)
Async XLA Ops:
  0.6 1.1 copy-start
  0.6 63.8 %copy-start.1 = (f32[128,2,2,512,1]{3,0,2,4,1:T(8,128)S(1)}, f32[128,2,2,512,1]{3,0,2,4,1:T(8,128)}, u32[]{:S(2)}) copy-start(f32[128,2,2,512,1]{3,0,2,4,1:T(8,128)} %constant.19) | copy-start | bytes 3145732
  0.7 63.8 %copy-start.3 = (s32[32,12]{0,1:T(8,128)S(1)}, s32[32,12]{0,1:T(8,128)}, u32[]{:S(2)}) copy-start(s32[32,12]{0,1:T(8,128)} %param.8) | copy-start | bytes 4612
  43.0 20.8 %all-to-all-start.1 = ((f32[128,1,1536]{2,1,0:T(1,128)}), f32[128,1,1536]{2,1,0:T(1,128)S(1)}, u32[]{:S(2)}, u32[]{:S(2)}) async-start(f32[128,1,1536]{2,1,0:T(1,128)} %bitcast.88), calls=%async_computation.1 | async-start | bytes 1572864 | tf_op jit(solution)/shard_map/all_to_all | solution.py:175
  65.2 61.2 %copy-start.2 = (f32[32,12,512]{2,0,1:T(8,128)}, f32[32,12,512]{2,0,1:T(8,128)S(1)}, u32[]{:S(2)}) copy-start(f32[32,12,512]{2,0,1:T(8,128)S(1)} %fusion.13) | copy-start | bytes 2359300

commit v10 on v8

--- a/solution.py
+++ b/solution.py
@@ -11,8 +11,8 @@
 
 NFREQ = 256
 NT = 512
-TS = 512
-TS_ADJ = 768
+TS = 256
+TS_ADJ = 512
 
 
 def _partner(x, negate_first):

time: 123 us -> 124 us (level)
  no operation moved by 1% of the time
where the time goes in v10:
time: 124 us; the launch traced here: 123 us
  blocking collectives  64.1 us (52%)
  Pallas kernels  22.3 us (18%)
  waiting for transfers between devices  16.2 us (13%)
  matrix products  8.29 us (7%)
  local copies, waits for them, and re-layouts  7.05 us (6%)
  starting transfers between devices  4.51 us (4%)
    all_to_all x2, blocking collectives, convolve(): arrived = lax.all_to_all(spectra, 'af', 0, 0, tiled=True)  43.1 us
    all_to_all x1, blocking collectives, convolve(): return lax.all_to_all(result, 'af', 0, 0, tiled=True)  21 us
    all_to_all x1, waiting for transfers between devices, convolve(): return lax.all_to_all(result, 'af', 0, 0, tiled=True)  16.2 us
    pallas_call x1, Pallas kernels, forward_kernel(): pl.pallas_call(_fwd_kernel, grid=(stations // TS,), in_specs=[pl.BlockSpe...  11.3 us
    pallas_call x1, Pallas kernels, adjoint_kernel(): pl.pallas_call(_adj_kernel, grid=(stations // TS_ADJ,), in_specs=[pl.Bloc...  11 us
    all_to_all x1, starting transfers between devices, convolve(): return lax.all_to_all(result, 'af', 0, 0, tiled=True)  4.51 us
    dot_general x2, matrix products, spectra_of(): jnp.einsum('pst,dqt->dsqp', traces, tab, precision=lax.Precision.HIGH, pr...  4.38 us
    dot_general x2, matrix products, traces_of(): lax.dot_general(spec, tab, (((0, 2, 3), (0, 1, 2)), ((), ())), precision=...  3.91 us
  transfers between devices with their start and end apart: 1, of which 1 were waited for; matrix products, arithmetic and copies ran while one was open for 0% of the time, Pallas kernels for 0%

profile of v10, /device:TPU:1, one launch (start us, length us, event | category | flops | bytes accessed | tf_op | source)
XLA Modules:
  0.0 123.3 jit_solution(12657153484535607492)
XLA Ops:
  0.6 0.0 copy-start
  0.6 0.0 copy-start.1
  0.7 0.0 copy-start.3
  0.7 1.1 copy-done
  1.8 2.0 %fusion.33 = bf16[128,12,4,32]{0,3,1,2:T(8,128)(2,1)S(1)} fusion(f32[128,4,512,1]{2,0,3,1:T(8,128)} %constant.18, f32[32,12,512]{2,0,1:T(8,128)S(1)} %copy-done), kind=kOutput, calls=%fused_computation.17 | convolution fusion | flops 604372992 | bytes 2228224 | tf_op jit(solution)/shard_map/pst,dqt->dsqp/dot_general | solution.py:115
  3.9 0.4 copy.21
  4.3 24.8 %all_to_all.20 = bf16[128,12,128]{2,1,0:T(8,128)(2,1)S(1)} all-to-all(bf16[128,12,128]{2,1,0:T(8,128)(2,1)S(1)} %copy.21), channel_id=1, replica_groups=mesh['af'=128] {'af'}, dimensions={0} | all-to-all | bytes 786432 | tf_op jit(solution)/shard_map/all_to_all | solution.py:153
  29.1 0.8 reshape.44.x_ref
  30.0 11.3 %shard_map.68 = f32[1536,128]{1,0:T(8,128)} custom-call(bf16[1536,128]{1,0:T(8,128)(2,1)} %reshape.44.x_ref, bf16[2,2,1536,1536]{3,2,1,0:T(8,128)(2,1)} %r_ref.3), custom_call_target="tpu_custom_call" | custom-call | tf_op jit(solution)/shard_map/pallas_call | solution.py:48
  41.3 4.5 %all-to-all-start.1 = ((f32[128,1,1536]{2,1,0:T(1,128)}), f32[128,1,1536]{2,1,0:T(1,128)S(1)}, u32[]{:S(2)}, u32[]{:S(2)}) async-start(f32[128,1,1536]{2,1,0:T(1,128)} %bitcast.88), calls=%async_computation.1 | async-start | bytes 1572864 | tf_op jit(solution)/shard_map/all_to_all | solution.py:157
  45.9 16.2 %all-to-all-done.1 = f32[128,1,1536]{2,1,0:T(1,128)S(1)} async-done(((f32[128,1,1536]{2,1,0:T(1,128)}), f32[128,1,1536]{2,1,0:T(1,128)S(1)}, u32[]{:S(2)}, u32[]{:S(2)}) %all-to-all-start.1) | async-done | bytes 786464 | tf_op jit(solution)/shard_map/all_to_all | solution.py:157
  62.1 0.6 copy.23
  62.7 0.0 copy-done.1
  62.7 0.0 copy-done.3
  62.7 0.8 fusion.13
  63.5 0.0 copy-start.2
  63.5 2.3 %fusion.32 = bf16[32,12,128,4]{2,0,3,1:T(8,128)(2,1)S(1)} fusion(f32[128,4,512,1]{2,0,1,3:T(8,128)} %constant.20, f32[32,12,512]{2,0,1:T(8,128)S(1)} %fusion.13), kind=kOutput, calls=%fused_computation.16 | convolution fusion | flops 604372992 | bytes 2228224 | tf_op jit(solution)/shard_map/pst,dqt->dsqp/dot_general | solution.py:115
  65.9 0.4 copy.25
  66.3 18.3 %all_to_all.21 = bf16[128,12,128]{2,1,0:T(8,128)(2,1)} all-to-all(bf16[128,12,128]{2,1,0:T(8,128)(2,1)S(1)} %copy.25), channel_id=1, replica_groups=mesh['af'=128] {'af'}, dimensions={0} | all-to-all | bytes 786432 | tf_op jit(solution)/shard_map/all_to_all | solution.py:153
  84.6 1.9 %reshape.49.y_ref = bf16[1536,128]{1,0:T(8,128)(2,1)} reshape(bf16[128,12,128]{2,1,0:T(8,128)(2,1)} %all_to_all.21) | data formatting | bytes 786432 | tf_op jit(solution)/shard_map/reshape | solution.py:155
  86.5 11.0 %shard_map.69 = f32[1536,128]{1,0:T(8,128)} custom-call(bf16[1536,128]{1,0:T(8,128)(2,1)} %reshape.49.y_ref, bf16[2,2,1536,1536]{3,2,1,0:T(8,128)(2,1)} %r_ref.3), custom_call_target="tpu_custom_call" | custom-call | tf_op jit(solution)/shard_map/pallas_call | solution.py:89
  97.4 21.0 %all_to_all.22 = f32[128,1,1536]{2,1,0:T(1,128)S(1)} all-to-all(f32[128,1,1536]{2,1,0:T(1,128)} %bitcast.89), channel_id=1, replica_groups=mesh['af'=128] {'af'}, dimensions={0} | all-to-all | bytes 1572864 | tf_op jit(solution)/shard_map/all_to_all | solution.py:157
  118.4 1.8 %copy.27 = f32[128,1,1536]{0,2,1:T(8,128)} copy(f32[128,1,1536]{2,1,0:T(1,128)S(1)} %all_to_all.22) | data formatting | bytes 1572864 | tf_op jit(solution)/shard_map/all_to_all | solution.py:157
  120.2 3.1 %fusion.28 = f32[32,12,512]{2,0,1:T(8,128)} fusion(f32[32,12,512]{2,0,1:T(8,128)} %param.7, f32[128,12,2,2,32]{0,4,3,2,1:T(8,128)} %bitcast.90, f32[128,2,2,512,1]{3,0,2,4,1:T(8,128)S(1)} %copy-done.1, s32[32,12]{0,1:T(8,128)S(1)} %copy-done.3, s32[512]{0:T(512)S(1)} %add_abs_fusion), kind=kOutput, calls=%fused_computation.14 | convolution fusion | flops 604766208 | bytes 3411456 | tf_op jit(solution)/shard_map/dot_general | solution.py:129
  123.3 0.0 copy-done.2
  (2 shorter events, 0.0 us)
Async XLA Ops:
  0.6 1.1 copy-start
  0.6 62.0 %copy-start.1 = (f32[128,2,2,512,1]{3,0,2,4,1:T(8,128)S(1)}, f32[128,2,2,512,1]{3,0,2,4,1:T(8,128)}, u32[]{:S(2)}) copy-start(f32[128,2,2,512,1]{3,0,2,4,1:T(8,128)} %constant.19) | copy-start | bytes 3145732
  0.7 62.0 %copy-start.3 = (s32[32,12]{0,1:T(8,128)S(1)}, s32[32,12]{0,1:T(8,128)}, u32[]{:S(2)}) copy-start(s32[32,12]{0,1:T(8,128)} %param.8) | copy-start | bytes 4612
  41.3 20.8 %all-to-all-start.1 = ((f32[128,1,1536]{2,1,0:T(1,128)}), f32[128,1,1536]{2,1,0:T(1,128)S(1)}, u32[]{:S(2)}, u32[]{:S(2)}) async-start(f32[128,1,1536]{2,1,0:T(1,128)} %bitcast.88), calls=%async_computation.1 | async-start | bytes 1572864 | tf_op jit(solution)/shard_map/all_to_all | solution.py:157
  63.5 59.8 %copy-start.2 = (f32[32,12,512]{2,0,1:T(8,128)}, f32[32,12,512]{2,0,1:T(8,128)S(1)}, u32[]{:S(2)}) copy-start(f32[32,12,512]{2,0,1:T(8,128)S(1)} %fusion.13) | copy-start | bytes 2359300

commit v11 on v10

--- a/solution.py
+++ b/solution.py
@@ -11,7 +11,7 @@
 
 NFREQ = 256
 NT = 512
-TS = 256
+TS = 768
 TS_ADJ = 512
 
 

time: 124 us -> 123 us (level)
  no operation moved by 1% of the time
where the time goes in v11:
time: 123 us; the launch traced here: 122 us
  blocking collectives  64.1 us (52%)
  Pallas kernels  21.1 us (17%)
  waiting for transfers between devices  16.2 us (13%)
  matrix products  8.29 us (7%)
  local copies, waits for them, and re-layouts  7.05 us (6%)
  starting transfers between devices  4.51 us (4%)
    all_to_all x2, blocking collectives, convolve(): arrived = lax.all_to_all(spectra, 'af', 0, 0, tiled=True)  43.1 us
    all_to_all x1, blocking collectives, convolve(): return lax.all_to_all(result, 'af', 0, 0, tiled=True)  21 us
    all_to_all x1, waiting for transfers between devices, convolve(): return lax.all_to_all(result, 'af', 0, 0, tiled=True)  16.2 us
    pallas_call x1, Pallas kernels, adjoint_kernel(): pl.pallas_call(_adj_kernel, grid=(stations // TS_ADJ,), in_specs=[pl.Bloc...  11 us
    pallas_call x1, Pallas kernels, forward_kernel(): pl.pallas_call(_fwd_kernel, grid=(stations // TS,), in_specs=[pl.BlockSpe...  10.2 us
    all_to_all x1, starting transfers between devices, convolve(): return lax.all_to_all(result, 'af', 0, 0, tiled=True)  4.51 us
    dot_general x2, matrix products, spectra_of(): jnp.einsum('pst,dqt->dsqp', traces, tab, precision=lax.Precision.HIGH, pr...  4.37 us
    dot_general x2, matrix products, traces_of(): lax.dot_general(spec, tab, (((0, 2, 3), (0, 1, 2)), ((), ())), precision=...  3.92 us
  transfers between devices with their start and end apart: 1, of which 1 were waited for; matrix products, arithmetic and copies ran while one was open for 0% of the time, Pallas kernels for 0%

profile of v11, /device:TPU:1, one launch (start us, length us, event | category | flops | bytes accessed | tf_op | source)
XLA Modules:
  0.0 122.1 jit_solution(9931322593227926272)
XLA Ops:
  0.6 0.0 copy-start
  0.6 0.0 copy-start.1
  0.7 0.0 copy-start.3
  0.7 1.1 copy-done
  1.8 2.0 %fusion.33 = bf16[128,12,4,32]{0,3,1,2:T(8,128)(2,1)S(1)} fusion(f32[128,4,512,1]{2,0,3,1:T(8,128)} %constant.18, f32[32,12,512]{2,0,1:T(8,128)S(1)} %copy-done), kind=kOutput, calls=%fused_computation.17 | convolution fusion | flops 604372992 | bytes 2228224 | tf_op jit(solution)/shard_map/pst,dqt->dsqp/dot_general | solution.py:115
  3.9 0.4 copy.21
  4.3 24.8 %all_to_all.20 = bf16[128,12,128]{2,1,0:T(8,128)(2,1)S(1)} all-to-all(bf16[128,12,128]{2,1,0:T(8,128)(2,1)S(1)} %copy.21), channel_id=1, replica_groups=mesh['af'=128] {'af'}, dimensions={0} | all-to-all | bytes 786432 | tf_op jit(solution)/shard_map/all_to_all | solution.py:153
  29.1 0.8 reshape.44.x_ref
  30.0 10.2 %shard_map.68 = f32[1536,128]{1,0:T(8,128)} custom-call(bf16[1536,128]{1,0:T(8,128)(2,1)} %reshape.44.x_ref, bf16[2,2,1536,1536]{3,2,1,0:T(8,128)(2,1)} %r_ref.3), custom_call_target="tpu_custom_call" | custom-call | tf_op jit(solution)/shard_map/pallas_call | solution.py:48
  40.1 4.5 %all-to-all-start.1 = ((f32[128,1,1536]{2,1,0:T(1,128)}), f32[128,1,1536]{2,1,0:T(1,128)S(1)}, u32[]{:S(2)}, u32[]{:S(2)}) async-start(f32[128,1,1536]{2,1,0:T(1,128)} %bitcast.88), calls=%async_computation.1 | async-start | bytes 1572864 | tf_op jit(solution)/shard_map/all_to_all | solution.py:157
  44.7 16.2 %all-to-all-done.1 = f32[128,1,1536]{2,1,0:T(1,128)S(1)} async-done(((f32[128,1,1536]{2,1,0:T(1,128)}), f32[128,1,1536]{2,1,0:T(1,128)S(1)}, u32[]{:S(2)}, u32[]{:S(2)}) %all-to-all-start.1) | async-done | bytes 786464 | tf_op jit(solution)/shard_map/all_to_all | solution.py:157
  60.9 0.6 copy.23
  61.5 0.0 copy-done.1
  61.5 0.0 copy-done.3
  61.5 0.8 fusion.13
  62.3 0.0 copy-start.2
  62.3 2.3 %fusion.32 = bf16[32,12,128,4]{2,0,3,1:T(8,128)(2,1)S(1)} fusion(f32[128,4,512,1]{2,0,1,3:T(8,128)} %constant.20, f32[32,12,512]{2,0,1:T(8,128)S(1)} %fusion.13), kind=kOutput, calls=%fused_computation.16 | convolution fusion | flops 604372992 | bytes 2228224 | tf_op jit(solution)/shard_map/pst,dqt->dsqp/dot_general | solution.py:115
  64.7 0.4 copy.25
  65.1 18.3 %all_to_all.21 = bf16[128,12,128]{2,1,0:T(8,128)(2,1)} all-to-all(bf16[128,12,128]{2,1,0:T(8,128)(2,1)S(1)} %copy.25), channel_id=1, replica_groups=mesh['af'=128] {'af'}, dimensions={0} | all-to-all | bytes 786432 | tf_op jit(solution)/shard_map/all_to_all | solution.py:153
  83.4 1.9 %reshape.49.y_ref = bf16[1536,128]{1,0:T(8,128)(2,1)} reshape(bf16[128,12,128]{2,1,0:T(8,128)(2,1)} %all_to_all.21) | data formatting | bytes 786432 | tf_op jit(solution)/shard_map/reshape | solution.py:155
  85.3 11.0 %shard_map.69 = f32[1536,128]{1,0:T(8,128)} custom-call(bf16[1536,128]{1,0:T(8,128)(2,1)} %reshape.49.y_ref, bf16[2,2,1536,1536]{3,2,1,0:T(8,128)(2,1)} %r_ref.3), custom_call_target="tpu_custom_call" | custom-call | tf_op jit(solution)/shard_map/pallas_call | solution.py:89
  96.2 21.0 %all_to_all.22 = f32[128,1,1536]{2,1,0:T(1,128)S(1)} all-to-all(f32[128,1,1536]{2,1,0:T(1,128)} %bitcast.89), channel_id=1, replica_groups=mesh['af'=128] {'af'}, dimensions={0} | all-to-all | bytes 1572864 | tf_op jit(solution)/shard_map/all_to_all | solution.py:157
  117.2 1.8 %copy.27 = f32[128,1,1536]{0,2,1:T(8,128)} copy(f32[128,1,1536]{2,1,0:T(1,128)S(1)} %all_to_all.22) | data formatting | bytes 1572864 | tf_op jit(solution)/shard_map/all_to_all | solution.py:157
  119.0 3.1 %fusion.28 = f32[32,12,512]{2,0,1:T(8,128)} fusion(f32[32,12,512]{2,0,1:T(8,128)} %param.7, f32[128,12,2,2,32]{0,4,3,2,1:T(8,128)} %bitcast.90, f32[128,2,2,512,1]{3,0,2,4,1:T(8,128)S(1)} %copy-done.1, s32[32,12]{0,1:T(8,128)S(1)} %copy-done.3, s32[512]{0:T(512)S(1)} %add_abs_fusion), kind=kOutput, calls=%fused_computation.14 | convolution fusion | flops 604766208 | bytes 3411456 | tf_op jit(solution)/shard_map/dot_general | solution.py:129
  122.1 0.0 copy-done.2
  (2 shorter events, 0.0 us)
Async XLA Ops:
  0.6 1.1 copy-start
  0.6 60.8 %copy-start.1 = (f32[128,2,2,512,1]{3,0,2,4,1:T(8,128)S(1)}, f32[128,2,2,512,1]{3,0,2,4,1:T(8,128)}, u32[]{:S(2)}) copy-start(f32[128,2,2,512,1]{3,0,2,4,1:T(8,128)} %constant.19) | copy-start | bytes 3145732
  0.7 60.8 %copy-start.3 = (s32[32,12]{0,1:T(8,128)S(1)}, s32[32,12]{0,1:T(8,128)}, u32[]{:S(2)}) copy-start(s32[32,12]{0,1:T(8,128)} %param.8) | copy-start | bytes 4612
  40.1 20.8 %all-to-all-start.1 = ((f32[128,1,1536]{2,1,0:T(1,128)}), f32[128,1,1536]{2,1,0:T(1,128)S(1)}, u32[]{:S(2)}, u32[]{:S(2)}) async-start(f32[128,1,1536]{2,1,0:T(1,128)} %bitcast.88), calls=%async_computation.1 | async-start | bytes 1572864 | tf_op jit(solution)/shard_map/all_to_all | solution.py:157
  62.3 59.8 %copy-start.2 = (f32[32,12,512]{2,0,1:T(8,128)}, f32[32,12,512]{2,0,1:T(8,128)S(1)}, u32[]{:S(2)}) copy-start(f32[32,12,512]{2,0,1:T(8,128)S(1)} %fusion.13) | copy-start | bytes 2359300

commit v12 on v7

--- a/solution.py
+++ b/solution.py
@@ -57,13 +57,12 @@
     )(x, reflection)
 
 
-def _adj_kernel(y_ref, r_ref, o_ref, yp_ref, acc_ref):
+def _adj_kernel(y_ref, r_ref, o_ref, yp_ref):
     i = pl.program_id(0)
 
     @pl.when(i == 0)
     def _():
         yp_ref[...] = _partner(y_ref[...], False)
-        acc_ref[...] = jnp.zeros(acc_ref.shape, jnp.float32)
 
     off = pl.multiple_of(i * TS, TS)
     y = y_ref[pl.ds(off, TS), :]
@@ -76,11 +75,15 @@
         a = a + lax.dot_general(r_ref[1, kl], yp[:, kl * 64:(kl + 1) * 64], dims,
                                 preferred_element_type=jnp.float32)
         parts.append(a)
-    acc_ref[...] += jnp.concatenate(parts, 1)
+    total = jnp.concatenate(parts, 1)
 
-    @pl.when(i == pl.num_programs(0) - 1)
+    @pl.when(i == 0)
     def _():
-        o_ref[...] = acc_ref[...]
+        o_ref[...] = total
+
+    @pl.when(i > 0)
+    def _():
+        o_ref[...] += total
 
 
 def adjoint_kernel(reflection, y):
@@ -96,7 +99,6 @@
         out_shape=jax.ShapeDtypeStruct((stations, 128), jnp.float32),
         scratch_shapes=[
             pltpu.VMEM((stations, 128), jnp.bfloat16),
-            pltpu.VMEM((stations, 128), jnp.float32),
         ],
     )(y, reflection)
 

time: 123 us -> 123 us (level)
  no operation moved by 1% of the time
where the time goes in v12:
time: 123 us; the launch traced here: 122 us
  blocking collectives  64.1 us (52%)
  Pallas kernels  21.5 us (17%)
  waiting for transfers between devices  16.2 us (13%)
  matrix products  8.29 us (7%)
  local copies, waits for them, and re-layouts  7.05 us (6%)
  starting transfers between devices  4.51 us (4%)
    all_to_all x2, blocking collectives, convolve(): arrived = lax.all_to_all(spectra, 'af', 0, 0, tiled=True)  43.1 us
    all_to_all x1, blocking collectives, convolve(): return lax.all_to_all(result, 'af', 0, 0, tiled=True)  21 us
    all_to_all x1, waiting for transfers between devices, convolve(): return lax.all_to_all(result, 'af', 0, 0, tiled=True)  16.2 us
    pallas_call x1, Pallas kernels, adjoint_kernel(): pl.pallas_call(_adj_kernel, grid=(stations // TS,), in_specs=[pl.BlockSpe...  11 us
    pallas_call x1, Pallas kernels, forward_kernel(): pl.pallas_call(_fwd_kernel, grid=(stations // TS,), in_specs=[pl.BlockSpe...  10.5 us
    all_to_all x1, starting transfers between devices, convolve(): return lax.all_to_all(result, 'af', 0, 0, tiled=True)  4.51 us
    dot_general x2, matrix products, spectra_of(): jnp.einsum('pst,dqt->dsqp', traces, tab, precision=lax.Precision.HIGH, pr...  4.38 us
    dot_general x2, matrix products, traces_of(): lax.dot_general(spec, tab, (((0, 2, 3), (0, 1, 2)), ((), ())), precision=...  3.91 us
  transfers between devices with their start and end apart: 1, of which 1 were waited for; matrix products, arithmetic and copies ran while one was open for 0% of the time, Pallas kernels for 0%

profile of v12, /device:TPU:1, one launch (start us, length us, event | category | flops | bytes accessed | tf_op | source)
XLA Modules:
  0.0 122.5 jit_solution(4953545137912810772)
XLA Ops:
  0.6 0.0 copy-start
  0.6 0.0 copy-start.1
  0.7 0.0 copy-start.3
  0.7 1.1 copy-done
  1.8 2.0 %fusion.33 = bf16[128,12,4,32]{0,3,1,2:T(8,128)(2,1)S(1)} fusion(f32[128,4,512,1]{2,0,3,1:T(8,128)} %constant.18, f32[32,12,512]{2,0,1:T(8,128)S(1)} %copy-done), kind=kOutput, calls=%fused_computation.17 | convolution fusion | flops 604372992 | bytes 2228224 | tf_op jit(solution)/shard_map/pst,dqt->dsqp/dot_general | solution.py:116
  3.9 0.4 copy.21
  4.3 24.8 %all_to_all.20 = bf16[128,12,128]{2,1,0:T(8,128)(2,1)S(1)} all-to-all(bf16[128,12,128]{2,1,0:T(8,128)(2,1)S(1)} %copy.21), channel_id=1, replica_groups=mesh['af'=128] {'af'}, dimensions={0} | all-to-all | bytes 786432 | tf_op jit(solution)/shard_map/all_to_all | solution.py:154
  29.1 0.8 reshape.44.x_ref
  30.0 10.5 %shard_map.68 = f32[1536,128]{1,0:T(8,128)} custom-call(bf16[1536,128]{1,0:T(8,128)(2,1)} %reshape.44.x_ref, bf16[2,2,1536,1536]{3,2,1,0:T(8,128)(2,1)} %r_ref.3), custom_call_target="tpu_custom_call" | custom-call | tf_op jit(solution)/shard_map/pallas_call | solution.py:47
  40.5 4.5 %all-to-all-start.1 = ((f32[128,1,1536]{2,1,0:T(1,128)}), f32[128,1,1536]{2,1,0:T(1,128)S(1)}, u32[]{:S(2)}, u32[]{:S(2)}) async-start(f32[128,1,1536]{2,1,0:T(1,128)} %bitcast.88), calls=%async_computation.1 | async-start | bytes 1572864 | tf_op jit(solution)/shard_map/all_to_all | solution.py:158
  45.0 16.2 %all-to-all-done.1 = f32[128,1,1536]{2,1,0:T(1,128)S(1)} async-done(((f32[128,1,1536]{2,1,0:T(1,128)}), f32[128,1,1536]{2,1,0:T(1,128)S(1)}, u32[]{:S(2)}, u32[]{:S(2)}) %all-to-all-start.1) | async-done | bytes 786464 | tf_op jit(solution)/shard_map/all_to_all | solution.py:158
  61.2 0.6 copy.23
  61.8 0.0 copy-done.1
  61.8 0.0 copy-done.3
  61.8 0.8 fusion.13
  62.7 0.0 copy-start.2
  62.7 2.3 %fusion.32 = bf16[32,12,128,4]{2,0,3,1:T(8,128)(2,1)S(1)} fusion(f32[128,4,512,1]{2,0,1,3:T(8,128)} %constant.20, f32[32,12,512]{2,0,1:T(8,128)S(1)} %fusion.13), kind=kOutput, calls=%fused_computation.16 | convolution fusion | flops 604372992 | bytes 2228224 | tf_op jit(solution)/shard_map/pst,dqt->dsqp/dot_general | solution.py:116
  65.0 0.4 copy.25
  65.4 18.3 %all_to_all.21 = bf16[128,12,128]{2,1,0:T(8,128)(2,1)} all-to-all(bf16[128,12,128]{2,1,0:T(8,128)(2,1)S(1)} %copy.25), channel_id=1, replica_groups=mesh['af'=128] {'af'}, dimensions={0} | all-to-all | bytes 786432 | tf_op jit(solution)/shard_map/all_to_all | solution.py:154
  83.7 1.9 %reshape.49.y_ref = bf16[1536,128]{1,0:T(8,128)(2,1)} reshape(bf16[128,12,128]{2,1,0:T(8,128)(2,1)} %all_to_all.21) | data formatting | bytes 786432 | tf_op jit(solution)/shard_map/reshape | solution.py:156
  85.6 11.0 %shard_map.69 = f32[1536,128]{1,0:T(8,128)} custom-call(bf16[1536,128]{1,0:T(8,128)(2,1)} %reshape.49.y_ref, bf16[2,2,1536,1536]{3,2,1,0:T(8,128)(2,1)} %r_ref.3), custom_call_target="tpu_custom_call" | custom-call | tf_op jit(solution)/shard_map/pallas_call | solution.py:91
  96.6 21.0 %all_to_all.22 = f32[128,1,1536]{2,1,0:T(1,128)S(1)} all-to-all(f32[128,1,1536]{2,1,0:T(1,128)} %bitcast.89), channel_id=1, replica_groups=mesh['af'=128] {'af'}, dimensions={0} | all-to-all | bytes 1572864 | tf_op jit(solution)/shard_map/all_to_all | solution.py:158
  117.6 1.8 %copy.27 = f32[128,1,1536]{0,2,1:T(8,128)} copy(f32[128,1,1536]{2,1,0:T(1,128)S(1)} %all_to_all.22) | data formatting | bytes 1572864 | tf_op jit(solution)/shard_map/all_to_all | solution.py:158
  119.4 3.1 %fusion.28 = f32[32,12,512]{2,0,1:T(8,128)} fusion(f32[32,12,512]{2,0,1:T(8,128)} %param.7, f32[128,12,2,2,32]{0,4,3,2,1:T(8,128)} %bitcast.90, f32[128,2,2,512,1]{3,0,2,4,1:T(8,128)S(1)} %copy-done.1, s32[32,12]{0,1:T(8,128)S(1)} %copy-done.3, s32[512]{0:T(512)S(1)} %add_abs_fusion), kind=kOutput, calls=%fused_computation.14 | convolution fusion | flops 604766208 | bytes 3411456 | tf_op jit(solution)/shard_map/dot_general | solution.py:130
  122.5 0.0 copy-done.2
  (2 shorter events, 0.0 us)
Async XLA Ops:
  0.6 1.1 copy-start
  0.6 61.2 %copy-start.1 = (f32[128,2,2,512,1]{3,0,2,4,1:T(8,128)S(1)}, f32[128,2,2,512,1]{3,0,2,4,1:T(8,128)}, u32[]{:S(2)}) copy-start(f32[128,2,2,512,1]{3,0,2,4,1:T(8,128)} %constant.19) | copy-start | bytes 3145732
  0.7 61.2 %copy-start.3 = (s32[32,12]{0,1:T(8,128)S(1)}, s32[32,12]{0,1:T(8,128)}, u32[]{:S(2)}) copy-start(s32[32,12]{0,1:T(8,128)} %param.8) | copy-start | bytes 4612
  40.5 20.8 %all-to-all-start.1 = ((f32[128,1,1536]{2,1,0:T(1,128)}), f32[128,1,1536]{2,1,0:T(1,128)S(1)}, u32[]{:S(2)}, u32[]{:S(2)}) async-start(f32[128,1,1536]{2,1,0:T(1,128)} %bitcast.88), calls=%async_computation.1 | async-start | bytes 1572864 | tf_op jit(solution)/shard_map/all_to_all | solution.py:158
  62.7 59.8 %copy-start.2 = (f32[32,12,512]{2,0,1:T(8,128)}, f32[32,12,512]{2,0,1:T(8,128)S(1)}, u32[]{:S(2)}) copy-start(f32[32,12,512]{2,0,1:T(8,128)S(1)} %fusion.13) | copy-start | bytes 2359300

commit v13 on v7

--- a/solution.py
+++ b/solution.py
@@ -27,18 +27,14 @@
     return out.astype(jnp.bfloat16)
 
 
-def _fwd_kernel(x_ref, r_ref, o_ref, xp_ref):
-    @pl.when(pl.program_id(0) == 0)
-    def _():
-        xp_ref[...] = _partner(x_ref[...], True)
-
+def _fwd_kernel(x_ref, r_ref, o_ref):
     parts = []
     for kl in range(2):
         x = x_ref[:, kl * 64:(kl + 1) * 64]
-        xp = xp_ref[:, kl * 64:(kl + 1) * 64]
         a = jnp.dot(r_ref[0, kl], x, preferred_element_type=jnp.float32)
-        a = a + jnp.dot(r_ref[1, kl], xp, preferred_element_type=jnp.float32)
-        parts.append(a)
+        b = jnp.dot(r_ref[1, kl], x, preferred_element_type=jnp.float32)
+        parts.append(a[:, 0:32] - b[:, 32:64])
+        parts.append(a[:, 32:64] + b[:, 0:32])
     o_ref[...] = jnp.concatenate(parts, 1)
 
 
@@ -53,7 +49,6 @@
         ],
         out_specs=pl.BlockSpec((TS, 128), lambda i: (i, 0)),
         out_shape=jax.ShapeDtypeStruct((stations, 128), jnp.float32),
-        scratch_shapes=[pltpu.VMEM((stations, 128), jnp.bfloat16)],
     )(x, reflection)
 
 

time: 123 us -> 123 us (level)
  no operation moved by 1% of the time
where the time goes in v13:
time: 123 us; the launch traced here: 122 us
  blocking collectives  64.1 us (52%)
  Pallas kernels  21.4 us (17%)
  waiting for transfers between devices  16.2 us (13%)
  matrix products  8.29 us (7%)
  local copies, waits for them, and re-layouts  7.05 us (6%)
  starting transfers between devices  4.51 us (4%)
    all_to_all x2, blocking collectives, convolve(): arrived = lax.all_to_all(spectra, 'af', 0, 0, tiled=True)  43.1 us
    all_to_all x1, blocking collectives, convolve(): return lax.all_to_all(result, 'af', 0, 0, tiled=True)  21 us
    all_to_all x1, waiting for transfers between devices, convolve(): return lax.all_to_all(result, 'af', 0, 0, tiled=True)  16.2 us
    pallas_call x1, Pallas kernels, adjoint_kernel(): pl.pallas_call(_adj_kernel, grid=(stations // TS,), in_specs=[pl.BlockSpe...  11 us
    pallas_call x1, Pallas kernels, forward_kernel(): pl.pallas_call(_fwd_kernel, grid=(stations // TS,), in_specs=[pl.BlockSpe...  10.4 us
    all_to_all x1, starting transfers between devices, convolve(): return lax.all_to_all(result, 'af', 0, 0, tiled=True)  4.51 us
    dot_general x2, matrix products, spectra_of(): jnp.einsum('pst,dqt->dsqp', traces, tab, precision=lax.Precision.HIGH, pr...  4.37 us
    dot_general x2, matrix products, traces_of(): lax.dot_general(spec, tab, (((0, 2, 3), (0, 1, 2)), ((), ())), precision=...  3.91 us
  transfers between devices with their start and end apart: 1, of which 1 were waited for; matrix products, arithmetic and copies ran while one was open for 0% of the time, Pallas kernels for 0%

profile of v13, /device:TPU:1, one launch (start us, length us, event | category | flops | bytes accessed | tf_op | source)
XLA Modules:
  0.0 122.4 jit_solution(14960418074228408363)
XLA Ops:
  0.6 0.0 copy-start
  0.6 0.0 copy-start.1
  0.7 0.0 copy-start.3
  0.7 1.1 copy-done
  1.8 2.0 %fusion.33 = bf16[128,12,4,32]{0,3,1,2:T(8,128)(2,1)S(1)} fusion(f32[128,4,512,1]{2,0,3,1:T(8,128)} %constant.18, f32[32,12,512]{2,0,1:T(8,128)S(1)} %copy-done), kind=kOutput, calls=%fused_computation.17 | convolution fusion | flops 604372992 | bytes 2228224 | tf_op jit(solution)/shard_map/pst,dqt->dsqp/dot_general | solution.py:109
  3.9 0.4 copy.21
  4.3 24.8 %all_to_all.20 = bf16[128,12,128]{2,1,0:T(8,128)(2,1)S(1)} all-to-all(bf16[128,12,128]{2,1,0:T(8,128)(2,1)S(1)} %copy.21), channel_id=1, replica_groups=mesh['af'=128] {'af'}, dimensions={0} | all-to-all | bytes 786432 | tf_op jit(solution)/shard_map/all_to_all | solution.py:147
  29.1 0.8 reshape.44.x_ref
  30.0 10.4 %shard_map.68 = f32[1536,128]{1,0:T(8,128)} custom-call(bf16[1536,128]{1,0:T(8,128)(2,1)} %reshape.44.x_ref, bf16[2,2,1536,1536]{3,2,1,0:T(8,128)(2,1)} %r_ref.3), custom_call_target="tpu_custom_call" | custom-call | tf_op jit(solution)/shard_map/pallas_call | solution.py:43
  40.4 4.5 %all-to-all-start.1 = ((f32[128,1,1536]{2,1,0:T(1,128)}), f32[128,1,1536]{2,1,0:T(1,128)S(1)}, u32[]{:S(2)}, u32[]{:S(2)}) async-start(f32[128,1,1536]{2,1,0:T(1,128)} %bitcast.88), calls=%async_computation.1 | async-start | bytes 1572864 | tf_op jit(solution)/shard_map/all_to_all | solution.py:151
  44.9 16.2 %all-to-all-done.1 = f32[128,1,1536]{2,1,0:T(1,128)S(1)} async-done(((f32[128,1,1536]{2,1,0:T(1,128)}), f32[128,1,1536]{2,1,0:T(1,128)S(1)}, u32[]{:S(2)}, u32[]{:S(2)}) %all-to-all-start.1) | async-done | bytes 786464 | tf_op jit(solution)/shard_map/all_to_all | solution.py:151
  61.2 0.6 copy.23
  61.7 0.0 copy-done.1
  61.7 0.0 copy-done.3
  61.7 0.8 fusion.13
  62.6 0.0 copy-start.2
  62.6 2.3 %fusion.32 = bf16[32,12,128,4]{2,0,3,1:T(8,128)(2,1)S(1)} fusion(f32[128,4,512,1]{2,0,1,3:T(8,128)} %constant.20, f32[32,12,512]{2,0,1:T(8,128)S(1)} %fusion.13), kind=kOutput, calls=%fused_computation.16 | convolution fusion | flops 604372992 | bytes 2228224 | tf_op jit(solution)/shard_map/pst,dqt->dsqp/dot_general | solution.py:109
  64.9 0.4 copy.25
  65.4 18.3 %all_to_all.21 = bf16[128,12,128]{2,1,0:T(8,128)(2,1)} all-to-all(bf16[128,12,128]{2,1,0:T(8,128)(2,1)S(1)} %copy.25), channel_id=1, replica_groups=mesh['af'=128] {'af'}, dimensions={0} | all-to-all | bytes 786432 | tf_op jit(solution)/shard_map/all_to_all | solution.py:147
  83.6 1.9 %reshape.49.y_ref = bf16[1536,128]{1,0:T(8,128)(2,1)} reshape(bf16[128,12,128]{2,1,0:T(8,128)(2,1)} %all_to_all.21) | data formatting | bytes 786432 | tf_op jit(solution)/shard_map/reshape | solution.py:149
  85.5 11.0 %shard_map.69 = f32[1536,128]{1,0:T(8,128)} custom-call(bf16[1536,128]{1,0:T(8,128)(2,1)} %reshape.49.y_ref, bf16[2,2,1536,1536]{3,2,1,0:T(8,128)(2,1)} %r_ref.3), custom_call_target="tpu_custom_call" | custom-call | tf_op jit(solution)/shard_map/pallas_call | solution.py:83
  96.5 21.0 %all_to_all.22 = f32[128,1,1536]{2,1,0:T(1,128)S(1)} all-to-all(f32[128,1,1536]{2,1,0:T(1,128)} %bitcast.89), channel_id=1, replica_groups=mesh['af'=128] {'af'}, dimensions={0} | all-to-all | bytes 1572864 | tf_op jit(solution)/shard_map/all_to_all | solution.py:151
  117.5 1.8 %copy.27 = f32[128,1,1536]{0,2,1:T(8,128)} copy(f32[128,1,1536]{2,1,0:T(1,128)S(1)} %all_to_all.22) | data formatting | bytes 1572864 | tf_op jit(solution)/shard_map/all_to_all | solution.py:151
  119.3 3.1 %fusion.28 = f32[32,12,512]{2,0,1:T(8,128)} fusion(f32[32,12,512]{2,0,1:T(8,128)} %param.7, f32[128,12,2,2,32]{0,4,3,2,1:T(8,128)} %bitcast.90, f32[128,2,2,512,1]{3,0,2,4,1:T(8,128)S(1)} %copy-done.1, s32[32,12]{0,1:T(8,128)S(1)} %copy-done.3, s32[512]{0:T(512)S(1)} %add_abs_fusion), kind=kOutput, calls=%fused_computation.14 | convolution fusion | flops 604766208 | bytes 3411456 | tf_op jit(solution)/shard_map/dot_general | solution.py:123
  122.4 0.0 copy-done.2
  (2 shorter events, 0.0 us)
Async XLA Ops:
  0.6 1.1 copy-start
  0.6 61.1 %copy-start.1 = (f32[128,2,2,512,1]{3,0,2,4,1:T(8,128)S(1)}, f32[128,2,2,512,1]{3,0,2,4,1:T(8,128)}, u32[]{:S(2)}) copy-start(f32[128,2,2,512,1]{3,0,2,4,1:T(8,128)} %constant.19) | copy-start | bytes 3145732
  0.7 61.1 %copy-start.3 = (s32[32,12]{0,1:T(8,128)S(1)}, s32[32,12]{0,1:T(8,128)}, u32[]{:S(2)}) copy-start(s32[32,12]{0,1:T(8,128)} %param.8) | copy-start | bytes 4612
  40.4 20.8 %all-to-all-start.1 = ((f32[128,1,1536]{2,1,0:T(1,128)}), f32[128,1,1536]{2,1,0:T(1,128)S(1)}, u32[]{:S(2)}, u32[]{:S(2)}) async-start(f32[128,1,1536]{2,1,0:T(1,128)} %bitcast.88), calls=%async_computation.1 | async-start | bytes 1572864 | tf_op jit(solution)/shard_map/all_to_all | solution.py:151
  62.6 59.8 %copy-start.2 = (f32[32,12,512]{2,0,1:T(8,128)}, f32[32,12,512]{2,0,1:T(8,128)S(1)}, u32[]{:S(2)}) copy-start(f32[32,12,512]{2,0,1:T(8,128)S(1)} %fusion.13) | copy-start | bytes 2359300
